TPU v7x, 128 devices: a whole 4x4x4 slice. The times are simulated.
128 devices in a mesh: seg: 16 (over x_hi, z, core), chan: 8 (over y, x_lo).
Axes of the slice: x: 4 (x_hi: 2, x_lo: 2; x = x_hi * 2 + x_lo), y: 4, z: 4, core: 2. Of those that a mesh axis runs over, the one named last changes fastest.
Arguments:
- signal: bfloat16 [4096, 32768], P('chan', 'seg'), may hold values from -64 to 64
- spatial: float32 [4096, 64], P('chan'), may hold values from -0.09375 to 0.09375
- temporal: float32 [64, 256], replicated, may hold values from -5 to 5
- start_codes: float32 [64, 32768], P(None, 'seg'), may hold values from -1.2 to 1.2
- thresholds: float32 [64], replicated, may hold values from 0.05 to 0.3
- step_sizes: float32 [64], replicated, may hold values from 0.03 to 0.1
- breaks: int32 [16], replicated, may hold values from 0 to 32767, as said below
Outputs:
- final_codes: float32 [64, 32768], P(None, 'seg')
- space_atoms: float32 [4096, 64], P('chan')
- time_atoms: float32 [64, 256], replicated
Inputs may be any that keep to these rules, and one draw needn't show every extreme that they name: `breaks`: Increasing; one break lies in each of the 16 equal stretches of the window.
All inputs are finite; a program needn't handle non-finite values.
Results may differ from a plain program's by a relative error of at most 0.0058.
Values may be sent and summed in bfloat16 or wider, within the bound.
No kernel may reach another device: no remote copies, remote signals or barrier semaphores. Data moves between devices by JAX's collectives and lax.ppermute only.
A program may use at most 128 MiB of HBM per device.

v0:
```python
import jax
import jax.numpy as jnp
from jax import lax
from jax.sharding import PartitionSpec as P

ITERS = 10
OUTER = 2
CHUNK = 5
GHOST_BLOCKS = 10


epsilon = 1e-06
highest = lax.Precision.HIGHEST


def passed_along(value, axis, steps):
    count = lax.axis_size(axis)
    leading, last = (max(0, -steps), min(count, count - steps))
    return lax.ppermute(value, axis, [(source, source + steps) for source in range(leading, last)])


def widened(rows, ghost):
    seg_len = rows.shape[1]
    from_left = passed_along(rows[:, seg_len - ghost :], "seg", 1)
    from_right = passed_along(rows[:, :ghost], "seg", -1)
    return jnp.concatenate([from_left, rows, from_right], axis=1)


def butterfly_sum(value, axis):
    count = lax.axis_size(axis)
    distance = 1
    while distance < count:
        partner = lax.ppermute(value, axis, [(i, i ^ distance) for i in range(count)])
        value = value + partner
        distance *= 2
    return value


def one_hot_skew(block_width, tap_span, transposed=False):
    shape = (tap_span, block_width, block_width)
    d = lax.broadcasted_iota(jnp.int32, shape, 0)
    m = lax.broadcasted_iota(jnp.int32, shape, 2 if transposed else 1)
    i = lax.broadcasted_iota(jnp.int32, shape, 1 if transposed else 2)
    hit = d == i - m + (block_width - 1)
    return jnp.where(hit, 1.0, 0.0).astype(jnp.bfloat16).reshape(tap_span, block_width * block_width)


def band_sums_matrix(block_width, tap_count, offset):
    shape = (block_width, block_width, tap_count)
    m = lax.broadcasted_iota(jnp.int32, shape, 0)
    i = lax.broadcasted_iota(jnp.int32, shape, 1)
    tau = lax.broadcasted_iota(jnp.int32, shape, 2)
    hit = tau == i - m + block_width * offset
    return jnp.where(hit, 1.0, 0.0).reshape(block_width * block_width, tap_count)


def toeplitz(kernel_taps, block_width, skew):
    atoms_here, tap_count = kernel_taps.shape
    zero_pad = jnp.zeros((atoms_here, block_width), kernel_taps.dtype)
    padded = jnp.concatenate([zero_pad, kernel_taps, zero_pad, zero_pad], axis=1)
    lag_blocks = tap_count // block_width
    tap_span = 2 * block_width
    bands = jnp.concatenate(
        [padded[:, off * block_width + 1 : off * block_width + 1 + tap_span] for off in range(lag_blocks + 1)],
        axis=0,
    )
    flat = jnp.dot(bands, skew, preferred_element_type=jnp.float32).astype(kernel_taps.dtype)
    flat = flat.reshape(lag_blocks + 1, atoms_here, block_width, block_width)
    return [flat[off] for off in range(lag_blocks + 1)]


def lag_sums(code_ext, others, block_width, tap_count):
    atoms_here, seg_len = others.shape
    block_count = seg_len // block_width
    lag_blocks = tap_count // block_width
    extended = code_ext.reshape(atoms_here, block_count + lag_blocks, block_width)
    others_blocks = others.reshape(atoms_here, block_count, block_width)
    total = jnp.zeros((atoms_here, tap_count), jnp.float32)
    for offset in range(lag_blocks + 1):
        window = extended[:, lag_blocks - offset : lag_blocks - offset + block_count]
        grad = jnp.einsum(
            "kbm,kbi->kmi", window, others_blocks, preferred_element_type=jnp.float32, precision=highest
        ).reshape(atoms_here, block_width * block_width)
        total = total + jnp.dot(grad, band_sums_matrix(block_width, tap_count, offset), precision=highest)
    return total


def convolve_blocks(matrices, code_rows, before, block_width):
    atoms_here, seg_len = code_rows.shape
    block_count = seg_len // block_width
    lag_blocks = len(matrices) - 1
    extended = jnp.concatenate([before, code_rows], axis=1).reshape(
        atoms_here, block_count + lag_blocks, block_width
    )
    summed = jnp.zeros((atoms_here, block_count, block_width), jnp.float32)
    for offset, matrix in enumerate(matrices):
        window = extended[:, lag_blocks - offset : lag_blocks - offset + block_count]
        summed = summed + jnp.einsum(
            "kbm,kmi->kbi", window, matrix, preferred_element_type=jnp.float32, precision=highest
        )
    return summed.reshape(atoms_here, seg_len)


def correlate_blocks(matrices, residual_b, after_rim, block_width):
    atoms_here, seg_len = residual_b.shape
    block_count = seg_len // block_width
    extended = jnp.concatenate([residual_b, after_rim], axis=1).reshape(
        atoms_here, block_count + len(matrices) - 1, block_width
    )
    summed = jnp.zeros((atoms_here, block_count, block_width), jnp.float32)
    for offset, matrix in enumerate(matrices):
        window = extended[:, offset : offset + block_count]
        summed = summed + jnp.einsum(
            "kbi,kim->kbm", window, matrix, preferred_element_type=jnp.float32, precision=highest
        )
    return summed.reshape(atoms_here, seg_len)


def reconstruct(matrices, latent_rows, block_width, tap_count):
    latent_b = latent_rows.astype(jnp.bfloat16)
    before = passed_along(latent_b[:, latent_b.shape[1] - tap_count :], "seg", 1)
    return (convolve_blocks(matrices, latent_b, before, block_width), before, latent_b)


def on_device(signal, spatial, temporal, start_codes, thresholds, step_sizes, breaks):
    chan_rows, seg_len = signal.shape
    atoms_all, tap_count = temporal.shape
    block_width = 128
    skew = one_hot_skew(block_width, 2 * block_width)
    skew_flipped = one_hot_skew(block_width, 2 * block_width, transposed=True)
    ghost = GHOST_BLOCKS * block_width
    wide_positions = lax.axis_index("seg") * seg_len - ghost + lax.iota(jnp.int32, seg_len + 2 * ghost)
    wide_crosses = (wide_positions[None, :] < breaks[:, None]) & (
        breaks[:, None] < wide_positions[None, :] + tap_count
    )
    inside = jnp.where(
        (wide_positions >= 0) & (wide_positions < seg_len * lax.axis_size("seg")), 1.0, 0.0
    ).astype(jnp.float32)
    allowed_wide = inside * jnp.where(jnp.any(wide_crosses, axis=0), 0.0, 1.0).astype(jnp.float32)
    zero_rim = jnp.zeros((atoms_all, tap_count), jnp.bfloat16)
    raw_start = butterfly_sum(jnp.dot(spatial.T, spatial, precision=highest), "chan")
    scaling = 1.0 / jnp.sqrt(jnp.diag(raw_start) + epsilon)
    space_loc = spatial * scaling[None, :]
    gram_matrix = raw_start * scaling[:, None] * scaling[None, :]
    kernel = temporal / jnp.sqrt(jnp.sum(temporal * temporal, axis=1, keepdims=True) + epsilon)
    latent = start_codes
    for sweep_index in range(OUTER):
        space_b = space_loc.astype(jnp.bfloat16)
        kernel_b = kernel.astype(jnp.bfloat16)
        projected = butterfly_sum(
            jnp.dot(space_b.T, signal, preferred_element_type=jnp.float32), "chan"
        )
        own_gram = gram_matrix

        def mix_atoms(rebuilt_part):
            return jnp.dot(own_gram, rebuilt_part, precision=highest)

        matrices = toeplitz(kernel_b, block_width, skew)
        flipped = toeplitz(kernel_b, block_width, skew_flipped)
        step_col = step_sizes[:, None]
        limit_col = (step_sizes * thresholds)[:, None]

        both_wide = widened(jnp.concatenate([projected, latent], axis=0), ghost)
        projected_wide = both_wide[:atoms_all]

        def shrink_step(iteration, carried):
            current, current_b = carried
            rebuilt = convolve_blocks(matrices, current_b, zero_rim, block_width)
            residual = (projected_wide - mix_atoms(rebuilt)) * inside[None, :]
            descent = correlate_blocks(flipped, residual.astype(jnp.bfloat16), zero_rim, block_width)
            stepped = current + step_col * descent
            shrunk = (
                allowed_wide[None, :]
                * jnp.sign(stepped)
                * jnp.maximum(jnp.abs(stepped) - limit_col, 0.0)
            )
            return (shrunk, shrunk.astype(jnp.bfloat16))

        for chunk in range(ITERS // CHUNK):
            wide = both_wide[atoms_all:] if chunk == 0 else widened(latent, ghost)
            wide, _ = lax.fori_loop(0, CHUNK, shrink_step, (wide, wide.astype(jnp.bfloat16)))
            latent = wide[:, ghost : ghost + seg_len]
        rebuilt, before, latent_b = reconstruct(matrices, latent, block_width, tap_count)
        rebuilt_b = rebuilt.astype(jnp.bfloat16)
        row_part = jnp.dot(rebuilt_b, signal.T, preferred_element_type=jnp.float32)
        others = projected - jnp.dot(
            gram_matrix - jnp.diag(jnp.diag(gram_matrix)), rebuilt, precision=highest
        )
        code_ext = jnp.concatenate([before, latent_b], axis=1)
        taps_part = lag_sums(code_ext, others, block_width, tap_count)
        cross_part = jnp.dot(rebuilt, rebuilt.T, precision=highest)
        joined = butterfly_sum(jnp.concatenate([row_part, cross_part, taps_part], axis=1), "seg")
        stats_rows = joined[:, :chan_rows].T
        cross_gram = joined[:, chan_rows : chan_rows + atoms_all]
        raw_kernel = joined[:, chan_rows + atoms_all :]
        raw_rows = stats_rows - jnp.dot(
            space_loc, cross_gram - jnp.diag(jnp.diag(cross_gram)), precision=highest
        )
        raw_gram = butterfly_sum(jnp.dot(raw_rows.T, raw_rows, precision=highest), "chan")
        scaling = 1.0 / jnp.sqrt(jnp.diag(raw_gram) + epsilon)
        space_loc = raw_rows * scaling[None, :]
        gram_matrix = raw_gram * scaling[:, None] * scaling[None, :]
        kernel = raw_kernel / jnp.sqrt(
            jnp.sum(raw_kernel * raw_kernel, axis=1, keepdims=True) + epsilon
        )
    return (latent, space_loc, kernel)


def solution(mesh):
    placed = (P("chan", "seg"), P("chan", None), P(), P(None, "seg"), P(), P(), P())
    return jax.shard_map(
        on_device,
        mesh=mesh,
        in_specs=placed,
        out_specs=(P(None, "seg"), P("chan", None), P()),
        check_vma=False,
    )
```

profile of v0, /device:TPU:4, one launch (start us, length us, event | category | flops | bytes accessed | tf_op | source)
XLA Modules:
  0.0 647.0 jit_solution(16433856140139095826)
XLA Ops:
  7.6 4.5 convolution_convert_fusion.3
  12.1 3.0 collective-permute-start.2
  15.1 2.5 collective-permute-done.2
  20.2 3.5 slice_bitcast_fusion.9
  32.9 8.6 %collective-permute-done.4 = f32[64,2048]{1,0:T(8,128)S(1)} collective-permute-done((f32[64,2048]{1,0:T(8,128)S(1)}, f32[64,2048]{1,0:T(8,128)S(1)}, u32[]{:S(2)}, u32[]{:S(2)}) %collective-permute-start.4) | collective-permute-done | bytes 524320 | tf_op jit(solution)/shard_map/ppermute | solution.py:33
  41.6 4.3 collective-permute-start.5
  58.4 7.7 %collective-permute-start.7 = (f32[128,1280]{1,0:T(8,128)S(1)}, f32[128,1280]{1,0:T(8,128)S(1)}, u32[]{:S(2)}, u32[]{:S(2)}) collective-permute-start(f32[128,1280]{1,0:T(8,128)S(1)} %get-tuple-element.600), channel_id=1, source_target_pairs={{8,0},{16,8},{24,16},{32,24},{40,32},{48,40},{56,48},{64,56},{72,6... | collective-permute-start | bytes 1966088 | tf_op jit(solution)/shard_map/ppermute | solution.py:19
  66.2 5.7 collective-permute-done.6
  76.6 74.7 %while.52 = (s32[]{:T(128)}, f32[64,4608]{1,0:T(8,128)}, bf16[64,4608]{1,0:T(8,128)(2,1)S(1)}, f32[4608]{0:T(1024)S(1)}, f32[64,1]{0,1:T(1,128)S(1)}, /*index=5*...) while((s32[]{:T(128)}, f32[64,4608]{1,0:T(8,128)}, ...), condition=%wide.region_3.4_spmd.clone, body=%wide.region_2.3_spmd.clone.sunk | while | flops 684218880 | bytes 87890792 | solution.py:181
  77.1 2.4 fusion.437
  84.2 2.4 fusion.440
  92.0 2.4 fusion.437
  107.0 2.4 fusion.437
  114.1 2.4 fusion.440
  121.9 2.4 fusion.437
  136.8 2.4 fusion.437
  155.1 7.6 %collective-permute-start.9 = (f32[64,1280]{1,0:T(8,128)S(1)}, f32[64,1280]{1,0:T(8,128)}, u32[]{:S(2)}, u32[]{:S(2)}) collective-permute-start(f32[64,1280]{1,0:T(8,128)S(1)} %get-tuple-element.596), channel_id=1, source_target_pairs={{8,0},{16,8},{24,16},{32,24},{40,32},{48,40},{56,48},{64,56},{72,6... | collective-permute-start | bytes 983048 | tf_op jit(solution)/shard_map/ppermute | solution.py:19
  170.4 74.7 %while.53 = (s32[]{:T(128)}, f32[64,4608]{1,0:T(8,128)}, bf16[64,4608]{1,0:T(8,128)(2,1)S(1)}, f32[4608]{0:T(1024)S(1)}, f32[64,1]{0,1:T(1,128)S(1)}, /*index=5*...) while((s32[]{:T(128)}, f32[64,4608]{1,0:T(8,128)}, ...), condition=%wide.region_5.6_spmd.clone, body=%wide.region_4.5_spmd.clone.sunk | while | flops 684218880 | bytes 87890792 | solution.py:181
  170.9 2.4 fusion.456
  185.8 2.4 fusion.456
  200.7 2.4 fusion.456
  207.9 2.4 fusion.459
  215.7 2.4 fusion.456
  230.6 2.4 fusion.456
  249.1 6.2 collective-permute-done.10
  268.6 7.5 %fusion.131 = f32[64,256]{1,0:T(8,128)S(1)} fusion(f32[64,128,128]{2,1,0:T(8,128)S(1)} %fusion.208), kind=kOutput, calls=%fused_computation.197 | convolution fusion | flops 3233808384 | bytes 4259840 | tf_op jit(solution)/shard_map/dot_general | solution.py:84
  276.1 10.3 %fusion.176 = f32[64,256]{1,0:T(8,128)S(1)} fusion(f32[64,256]{1,0:T(8,128)S(1)} %fusion.131, f32[64,128,128]{2,1,0:T(8,128)S(1)} %fusion.204), kind=kOutput, calls=%fused_computation.206 | convolution fusion | flops 3238019072 | bytes 4325376 | tf_op jit(solution)/shard_map/dot_general | solution.py:84
  286.3 8.3 %fusion.166 = f32[64,256]{1,0:T(8,128)S(1)} fusion(f32[64,256]{1,0:T(8,128)S(1)} %fusion.176, f32[64,128,128]{2,1,0:T(8,128)S(1)} %fusion.201), kind=kOutput, calls=%fused_computation.204 | convolution fusion | flops 3238019072 | bytes 4325376 | tf_op jit(solution)/shard_map/dot_general | solution.py:84
  296.5 7.6 %collective-permute-done.12 = f32[64,832]{1,0:T(8,128)S(1)} collective-permute-done((f32[64,832]{1,0:T(8,128)S(1)}, f32[64,832]{1,0:T(8,128)S(1)}, u32[]{:S(2)}, u32[]{:S(2)}) %collective-permute-start.12) | collective-permute-done | bytes 213024 | tf_op jit(solution)/shard_map/ppermute | solution.py:33
  304.3 8.3 %collective-permute-done.13 = f32[64,832]{1,0:T(8,128)S(1)} collective-permute-done((f32[64,832]{1,0:T(8,128)S(1)}, f32[64,832]{1,0:T(8,128)S(1)}, u32[]{:S(2)}, u32[]{:S(2)}) %collective-permute-start.13) | collective-permute-done | bytes 213024 | tf_op jit(solution)/shard_map/ppermute | solution.py:33
  312.7 7.5 %collective-permute-done.14 = f32[64,832]{1,0:T(8,128)S(1)} collective-permute-done((f32[64,832]{1,0:T(8,128)S(1)}, f32[64,832]{1,0:T(8,128)S(1)}, u32[]{:S(2)}, u32[]{:S(2)}) %collective-permute-start.14) | collective-permute-done | bytes 213024 | tf_op jit(solution)/shard_map/ppermute | solution.py:33
  322.6 3.3 collective-permute-done.15
  329.9 2.7 collective-permute-start.17
  332.8 2.5 collective-permute-done.17
  338.4 7.5 %collective-permute-done.18 = f32[64,2048]{1,0:T(8,128)S(1)} collective-permute-done((f32[64,2048]{1,0:T(8,128)S(1)}, f32[64,2048]{1,0:T(8,128)S(1)}, u32[]{:S(2)}, u32[]{:S(2)}) %collective-permute-start.18) | collective-permute-done | bytes 524320 | tf_op jit(solution)/shard_map/ppermute | solution.py:33
  355.4 3.2 collective-permute-done.19
  358.6 3.7 collective-permute-start.20
  364.2 5.3 collective-permute-done.20
  371.6 7.7 %collective-permute-start.22 = (f32[128,1280]{1,0:T(8,128)S(1)}, f32[128,1280]{1,0:T(8,128)S(1)}, u32[]{:S(2)}, u32[]{:S(2)}) collective-permute-start(f32[128,1280]{1,0:T(8,128)S(1)} %get-tuple-element.598), channel_id=1, source_target_pairs={{8,0},{16,8},{24,16},{32,24},{40,32},{48,40},{56,48},{64,56},{72,6... | collective-permute-start | bytes 1966088 | tf_op jit(solution)/shard_map/ppermute | solution.py:19
  388.8 74.7 %while.54 = (s32[]{:T(128)}, f32[64,4608]{1,0:T(8,128)}, bf16[64,4608]{1,0:T(8,128)(2,1)S(1)}, f32[4608]{0:T(1024)S(1)}, f32[64,1]{0,1:T(1,128)S(1)}, /*index=5*...) while((s32[]{:T(128)}, f32[64,4608]{1,0:T(8,128)}, ...), condition=%wide.region_8.9_spmd.clone, body=%wide.region_7.8_spmd.clone.sunk | while | flops 684218880 | bytes 87890792 | solution.py:181
  389.3 2.4 fusion.475
  404.2 2.4 fusion.475
  419.1 2.4 fusion.475
  434.1 2.4 fusion.475
  449.0 2.4 fusion.475
  466.6 7.6 %collective-permute-start.24 = (f32[64,1280]{1,0:T(8,128)S(1)}, f32[64,1280]{1,0:T(8,128)S(1)}, u32[]{:S(2)}, u32[]{:S(2)}) collective-permute-start(f32[64,1280]{1,0:T(8,128)S(1)} %get-tuple-element.594), channel_id=1, source_target_pairs={{8,0},{16,8},{24,16},{32,24},{40,32},{48,40},{56,48},{64,56},{72,6... | collective-permute-start | bytes 983048 | tf_op jit(solution)/shard_map/ppermute | solution.py:19
  479.8 74.7 %while.55 = (s32[]{:T(128)}, f32[64,4608]{1,0:T(8,128)}, bf16[64,4608]{1,0:T(8,128)(2,1)S(1)}, f32[4608]{0:T(1024)S(1)}, f32[64,1]{0,1:T(1,128)S(1)}, /*index=5*...) while((s32[]{:T(128)}, f32[64,4608]{1,0:T(8,128)}, ...), condition=%wide.region_10.11_spmd.clone, body=%wide.region_9.10_spmd.clone.sunk | while | flops 684218880 | bytes 87890792 | solution.py:181
  480.2 2.4 fusion.494
  495.1 2.4 fusion.494
  502.3 2.4 fusion.497
  510.1 2.4 fusion.494
  525.0 2.4 fusion.494
  539.9 2.4 fusion.494
  547.0 2.4 fusion.497
  559.3 6.1 collective-permute-done.25
  578.6 7.5 %fusion.136 = f32[64,256]{1,0:T(8,128)S(1)} fusion(f32[64,128,128]{2,1,0:T(8,128)S(1)} %fusion.198), kind=kOutput, calls=%fused_computation.198 | convolution fusion | flops 3233808384 | bytes 4259840 | tf_op jit(solution)/shard_map/dot_general | solution.py:84
  586.1 10.3 %fusion.171 = f32[64,256]{1,0:T(8,128)S(1)} fusion(f32[64,256]{1,0:T(8,128)S(1)} %fusion.136, f32[64,128,128]{2,1,0:T(8,128)S(1)} %fusion.194), kind=kOutput, calls=%fused_computation.205 | convolution fusion | flops 3238019072 | bytes 4325376 | tf_op jit(solution)/shard_map/dot_general | solution.py:84
  596.4 8.3 %fusion.161 = f32[64,256]{1,0:T(8,128)S(1)} fusion(f32[64,256]{1,0:T(8,128)S(1)} %fusion.171, f32[64,128,128]{2,1,0:T(8,128)S(1)} %fusion.191), kind=kOutput, calls=%fused_computation.203 | convolution fusion | flops 3238019072 | bytes 4325376 | tf_op jit(solution)/shard_map/dot_general | solution.py:84
  606.5 7.6 %collective-permute-done.27 = f32[64,832]{1,0:T(8,128)S(1)} collective-permute-done((f32[64,832]{1,0:T(8,128)S(1)}, f32[64,832]{1,0:T(8,128)S(1)}, u32[]{:S(2)}, u32[]{:S(2)}) %collective-permute-start.27) | collective-permute-done | bytes 213024 | tf_op jit(solution)/shard_map/ppermute | solution.py:33
  614.3 8.3 %collective-permute-done.28 = f32[64,832]{1,0:T(8,128)S(1)} collective-permute-done((f32[64,832]{1,0:T(8,128)S(1)}, f32[64,832]{1,0:T(8,128)S(1)}, u32[]{:S(2)}, u32[]{:S(2)}) %collective-permute-start.28) | collective-permute-done | bytes 213024 | tf_op jit(solution)/shard_map/ppermute | solution.py:33
  622.7 7.5 %collective-permute-done.29 = f32[64,832]{1,0:T(8,128)S(1)} collective-permute-done((f32[64,832]{1,0:T(8,128)S(1)}, f32[64,832]{1,0:T(8,128)S(1)}, u32[]{:S(2)}, u32[]{:S(2)}) %collective-permute-start.29) | collective-permute-done | bytes 213024 | tf_op jit(solution)/shard_map/ppermute | solution.py:33
  633.3 2.5 collective-permute-done.30
  636.6 3.2 collective-permute-done.31
  639.8 3.4 collective-permute-start.32
  (734 shorter events, 371.1 us)
Async XLA Ops:
  0.6 17.8 %copy-start = (bf16[512,2048]{1,0:T(8,128)(2,1)S(1)}, bf16[512,2048]{1,0:T(8,128)(2,1)}, u32[]{:S(2)}) copy-start(bf16[512,2048]{1,0:T(8,128)(2,1)} %param.15) | copy-start | bytes 6291460
  2.0 4.0 collective-permute-start
  3.3 8.8 %copy-start.44 = (s32[16384]{0:T(1024)}, s32[16384]{0:T(1024)S(1)}, u32[]{:S(2)}) copy-start(s32[16384]{0:T(1024)S(1)} %add_bitcast_fusion.1) | copy-start | bytes 196612
  6.0 6.1 collective-permute-start.1
  7.6 10.8 %copy-start.39 = (f32[512,64]{0,1:T(8,128)S(1)}, f32[512,64]{0,1:T(8,128)}, u32[]{:S(2)}) copy-start(f32[512,64]{0,1:T(8,128)} %param.16) | copy-start | bytes 393220
  12.1 5.5 collective-permute-start.2
  18.4 47.7 %copy-start.50 = (f32[64]{0:T(128)}, f32[64]{0:T(128)S(1)}, u32[]{:S(2)}) copy-start(f32[64]{0:T(128)S(1)} %add_rsqrt_fusion.2) | copy-start | bytes 772
  19.0 11.5 %collective-permute-start.3 = (f32[64,2048]{1,0:T(8,128)S(1)}, f32[64,2048]{1,0:T(8,128)S(1)}, u32[]{:S(2)}, u32[]{:S(2)}) collective-permute-start(f32[64,2048]{1,0:T(8,128)S(1)} %fusion.221), channel_id=1, source_target_pairs={{0,1},{1,0},{2,3},{3,2},{4,5},{5,4},{6,7},{7,6},{8,9},{9,8},{10,11... | collective-permute-start | bytes 1572872 | tf_op jit(solution)/shard_map/ppermute | solution.py:33
  29.4 3.4 copy-start.46
  30.5 11.0 %collective-permute-start.4 = (f32[64,2048]{1,0:T(8,128)S(1)}, f32[64,2048]{1,0:T(8,128)S(1)}, u32[]{:S(2)}, u32[]{:S(2)}) collective-permute-start(f32[64,2048]{1,0:T(8,128)S(1)} %add.325), channel_id=1, source_target_pairs={{0,2},{1,3},{2,0},{3,1},{4,6},{5,7},{6,4},{7,5},{8,10},{9,11},{10,... | collective-permute-start | bytes 1572872 | tf_op jit(solution)/shard_map/ppermute | solution.py:33
  41.6 12.4 %collective-permute-start.5 = (f32[64,2048]{1,0:T(8,128)S(1)}, f32[64,2048]{1,0:T(8,128)}, u32[]{:S(2)}, u32[]{:S(2)}) collective-permute-start(f32[64,2048]{1,0:T(8,128)S(1)} %add.326), channel_id=1, source_target_pairs={{0,4},{1,5},{2,6},{3,7},{4,0},{5,1},{6,2},{7,3},{8,12},{9,13},{10,... | collective-permute-start | bytes 1572872 | tf_op jit(solution)/shard_map/ppermute | solution.py:33
  52.4 13.7 %copy-start.43 = (f32[64]{0:T(128)S(1)}, f32[64]{0:T(128)}, u32[]{:S(2)}) copy-start(f32[64]{0:T(128)} %param.20) | copy-start | bytes 772
  52.4 13.7 %copy-start.53 = (f32[64]{0:T(128)S(1)}, f32[64]{0:T(128)}, u32[]{:S(2)}) copy-start(f32[64]{0:T(128)} %param.19) | copy-start | bytes 772
  55.1 19.9 %copy-start.35 = (f32[64,2048]{1,0:T(8,128)}, f32[64,2048]{1,0:T(8,128)S(1)}, u32[]{:S(2)}) copy-start(f32[64,2048]{1,0:T(8,128)S(1)} %add.327) | copy-start | bytes 1572868
  56.4 15.5 %collective-permute-start.6 = (f32[128,1280]{1,0:T(8,128)S(1)}, f32[128,1280]{1,0:T(8,128)S(1)}, u32[]{:S(2)}, u32[]{:S(2)}) collective-permute-start(f32[128,1280]{1,0:T(8,128)S(1)} %get-tuple-element.599), channel_id=1, source_target_pairs={{0,8},{8,16},{16,24},{24,32},{32,40},{40,48},{48,56},{56,64},{64,7... | collective-permute-start | bytes 1966088 | tf_op jit(solution)/shard_map/ppermute | solution.py:19
  58.4 15.3 %collective-permute-start.7 = (f32[128,1280]{1,0:T(8,128)S(1)}, f32[128,1280]{1,0:T(8,128)S(1)}, u32[]{:S(2)}, u32[]{:S(2)}) collective-permute-start(f32[128,1280]{1,0:T(8,128)S(1)} %get-tuple-element.600), channel_id=1, source_target_pairs={{8,0},{16,8},{24,16},{32,24},{40,32},{48,40},{56,48},{64,56},{72,6... | collective-permute-start | bytes 1966088 | tf_op jit(solution)/shard_map/ppermute | solution.py:19
  77.1 2.4 copy-start.6
  92.0 2.4 copy-start.6
  106.9 2.4 copy-start.6
  121.9 2.4 copy-start.6
  136.8 2.4 copy-start.6
  153.2 12.4 %collective-permute-start.8 = (f32[64,1280]{1,0:T(8,128)}, f32[64,1280]{1,0:T(8,128)S(1)}, u32[]{:S(2)}, u32[]{:S(2)}) collective-permute-start(f32[64,1280]{1,0:T(8,128)} %get-tuple-element.595), channel_id=1, source_target_pairs={{0,8},{8,16},{16,24},{24,32},{32,40},{40,48},{48,56},{56,64},{64,7... | collective-permute-start | bytes 983048 | tf_op jit(solution)/shard_map/ppermute | solution.py:19
  155.1 12.0 %collective-permute-start.9 = (f32[64,1280]{1,0:T(8,128)S(1)}, f32[64,1280]{1,0:T(8,128)}, u32[]{:S(2)}, u32[]{:S(2)}) collective-permute-start(f32[64,1280]{1,0:T(8,128)S(1)} %get-tuple-element.596), channel_id=1, source_target_pairs={{8,0},{16,8},{24,16},{32,24},{40,32},{48,40},{56,48},{64,56},{72,6... | collective-permute-start | bytes 983048 | tf_op jit(solution)/shard_map/ppermute | solution.py:19
  185.8 2.4 copy-start.7
  200.7 2.4 copy-start.7
  230.6 2.4 copy-start.7
  246.2 9.1 %collective-permute-start.10 = (bf16[64,256]{1,0:T(8,128)(2,1)S(1)}, bf16[64,256]{1,0:T(8,128)(2,1)S(1)}, u32[]{:S(2)}, u32[]{:S(2)}) collective-permute-start(bf16[64,256]{1,0:T(8,128)(2,1)S(1)} %slice.370), channel_id=1, source_target_pairs={{0,8},{8,16},{16,24},{24,32},{32,40},{40,48},{48,56},{56,64},{64,7... | collective-permute-start | bytes 98312 | tf_op jit(solution)/shard_map/ppermute | solution.py:19
  294.6 26.4 %copy-start.40 = (f32[512,64]{0,1:T(8,128)S(1)}, f32[512,64]{0,1:T(8,128)}, u32[]{:S(2)}) copy-start(f32[512,64]{0,1:T(8,128)} %param.16) | copy-start | bytes 393220
  294.6 26.4 %copy-start.51 = (f32[64]{0:T(128)S(1)}, f32[64]{0:T(128)}, u32[]{:S(2)}) copy-start(f32[64]{0:T(128)} %copy-done.50) | copy-start | bytes 772
  294.7 1.6 collective-permute-start.11
  296.4 7.7 %collective-permute-start.12 = (f32[64,832]{1,0:T(8,128)S(1)}, f32[64,832]{1,0:T(8,128)S(1)}, u32[]{:S(2)}, u32[]{:S(2)}) collective-permute-start(f32[64,832]{1,0:T(8,128)S(1)} %fusion.282), channel_id=1, source_target_pairs={{0,16},{8,24},{16,0},{24,8},{32,48},{40,56},{48,32},{56,40},{64,80... | collective-permute-start | bytes 638984 | tf_op jit(solution)/shard_map/ppermute | solution.py:33
  304.2 8.4 %collective-permute-start.13 = (f32[64,832]{1,0:T(8,128)S(1)}, f32[64,832]{1,0:T(8,128)S(1)}, u32[]{:S(2)}, u32[]{:S(2)}) collective-permute-start(f32[64,832]{1,0:T(8,128)S(1)} %add.344), channel_id=1, source_target_pairs={{0,32},{8,40},{16,48},{24,56},{32,0},{40,8},{48,16},{56,24},{64,96... | collective-permute-start | bytes 638984 | tf_op jit(solution)/shard_map/ppermute | solution.py:33
  312.6 7.6 %collective-permute-start.14 = (f32[64,832]{1,0:T(8,128)S(1)}, f32[64,832]{1,0:T(8,128)S(1)}, u32[]{:S(2)}, u32[]{:S(2)}) collective-permute-start(f32[64,832]{1,0:T(8,128)S(1)} %add.345), channel_id=1, source_target_pairs={{0,64},{8,72},{16,80},{24,88},{32,96},{40,104},{48,112},{56,120},{... | collective-permute-start | bytes 638984 | tf_op jit(solution)/shard_map/ppermute | solution.py:33
  320.2 12.5 %copy-start.42 = (f32[64,832]{1,0:T(8,128)}, f32[64,832]{1,0:T(8,128)S(1)}, u32[]{:S(2)}) copy-start(f32[64,832]{1,0:T(8,128)S(1)} %add.346) | copy-start | bytes 638980
  321.5 15.2 %copy-start.37 = (f32[512,64]{0,1:T(8,128)}, f32[512,64]{0,1:T(8,128)S(1)}, u32[]{:S(2)}) copy-start(f32[512,64]{0,1:T(8,128)S(1)} %fusion.212) | copy-start | bytes 393220
  321.7 4.2 collective-permute-start.15
  326.0 3.9 collective-permute-start.16
  329.9 5.4 collective-permute-start.17
  336.1 49.5 %copy-start.48 = (f32[64]{0:T(128)}, f32[64]{0:T(128)S(1)}, u32[]{:S(2)}) copy-start(f32[64]{0:T(128)S(1)} %add_rsqrt_fusion.1) | copy-start | bytes 772
  336.1 10.9 %copy-start.47 = (s32[16384]{0:T(1024)S(1)}, s32[16384]{0:T(1024)}, u32[]{:S(2)}) copy-start(s32[16384]{0:T(1024)} %copy-done.46) | copy-start | bytes 196612
  336.7 9.3 %collective-permute-start.18 = (f32[64,2048]{1,0:T(8,128)S(1)}, f32[64,2048]{1,0:T(8,128)S(1)}, u32[]{:S(2)}, u32[]{:S(2)}) collective-permute-start(f32[64,2048]{1,0:T(8,128)S(1)} %fusion.222), channel_id=1, source_target_pairs={{0,1},{1,0},{2,3},{3,2},{4,5},{5,4},{6,7},{7,6},{8,9},{9,8},{10,11... | collective-permute-start | bytes 1572872 | tf_op jit(solution)/shard_map/ppermute | solution.py:33
  346.0 12.5 %collective-permute-start.19 = (f32[64,2048]{1,0:T(8,128)S(1)}, f32[64,2048]{1,0:T(8,128)S(1)}, u32[]{:S(2)}, u32[]{:S(2)}) collective-permute-start(f32[64,2048]{1,0:T(8,128)S(1)} %add.351), channel_id=1, source_target_pairs={{0,2},{1,3},{2,0},{3,1},{4,6},{5,7},{6,4},{7,5},{8,10},{9,11},{10,... | collective-permute-start | bytes 1572872 | tf_op jit(solution)/shard_map/ppermute | solution.py:33
  353.4 9.0 %copy-start.45 = (s32[16384]{0:T(1024)S(1)}, s32[16384]{0:T(1024)}, u32[]{:S(2)}) copy-start(s32[16384]{0:T(1024)} %copy-done.44) | copy-start | bytes 196612
  358.6 10.9 %collective-permute-start.20 = (f32[64,2048]{1,0:T(8,128)S(1)}, f32[64,2048]{1,0:T(8,128)S(1)}, u32[]{:S(2)}, u32[]{:S(2)}) collective-permute-start(f32[64,2048]{1,0:T(8,128)S(1)} %add.352), channel_id=1, source_target_pairs={{0,4},{1,5},{2,6},{3,7},{4,0},{5,1},{6,2},{7,3},{8,12},{9,13},{10,... | collective-permute-start | bytes 1572872 | tf_op jit(solution)/shard_map/ppermute | solution.py:33
  369.6 17.4 %copy-start.33 = (f32[64,2048]{1,0:T(8,128)}, f32[64,2048]{1,0:T(8,128)S(1)}, u32[]{:S(2)}) copy-start(f32[64,2048]{1,0:T(8,128)S(1)} %add.353) | copy-start | bytes 1572868
  369.7 16.0 %collective-permute-start.21 = (f32[128,1280]{1,0:T(8,128)S(1)}, f32[128,1280]{1,0:T(8,128)S(1)}, u32[]{:S(2)}, u32[]{:S(2)}) collective-permute-start(f32[128,1280]{1,0:T(8,128)S(1)} %get-tuple-element.597), channel_id=1, source_target_pairs={{0,8},{8,16},{16,24},{24,32},{32,40},{40,48},{48,56},{56,64},{64,7... | collective-permute-start | bytes 1966088 | tf_op jit(solution)/shard_map/ppermute | solution.py:19
  371.6 15.3 %collective-permute-start.22 = (f32[128,1280]{1,0:T(8,128)S(1)}, f32[128,1280]{1,0:T(8,128)S(1)}, u32[]{:S(2)}, u32[]{:S(2)}) collective-permute-start(f32[128,1280]{1,0:T(8,128)S(1)} %get-tuple-element.598), channel_id=1, source_target_pairs={{8,0},{16,8},{24,16},{32,24},{40,32},{48,40},{56,48},{64,56},{72,6... | collective-permute-start | bytes 1966088 | tf_op jit(solution)/shard_map/ppermute | solution.py:19
  449.0 2.4 copy-start.11
  464.6 12.2 %collective-permute-start.23 = (f32[64,1280]{1,0:T(8,128)S(1)}, f32[64,1280]{1,0:T(8,128)S(1)}, u32[]{:S(2)}, u32[]{:S(2)}) collective-permute-start(f32[64,1280]{1,0:T(8,128)S(1)} %get-tuple-element.593), channel_id=1, source_target_pairs={{0,8},{8,16},{16,24},{24,32},{32,40},{40,48},{48,56},{56,64},{64,7... | collective-permute-start | bytes 983048 | tf_op jit(solution)/shard_map/ppermute | solution.py:19
  466.6 12.0 %collective-permute-start.24 = (f32[64,1280]{1,0:T(8,128)S(1)}, f32[64,1280]{1,0:T(8,128)S(1)}, u32[]{:S(2)}, u32[]{:S(2)}) collective-permute-start(f32[64,1280]{1,0:T(8,128)S(1)} %get-tuple-element.594), channel_id=1, source_target_pairs={{8,0},{16,8},{24,16},{32,24},{40,32},{48,40},{56,48},{64,56},{72,6... | collective-permute-start | bytes 983048 | tf_op jit(solution)/shard_map/ppermute | solution.py:19
  480.2 2.4 copy-start.12
  495.1 2.4 copy-start.12
  525.0 2.4 copy-start.12
  539.9 2.4 copy-start.12
  556.3 9.0 %collective-permute-start.25 = (bf16[64,256]{1,0:T(8,128)(2,1)S(1)}, bf16[64,256]{1,0:T(8,128)(2,1)S(1)}, u32[]{:S(2)}, u32[]{:S(2)}) collective-permute-start(bf16[64,256]{1,0:T(8,128)(2,1)S(1)} %slice.387), channel_id=1, source_target_pairs={{0,8},{8,16},{16,24},{24,32},{32,40},{40,48},{48,56},{56,64},{64,7... | collective-permute-start | bytes 98312 | tf_op jit(solution)/shard_map/ppermute | solution.py:19
  604.6 26.4 %copy-start.38 = (f32[512,64]{0,1:T(8,128)S(1)}, f32[512,64]{0,1:T(8,128)}, u32[]{:S(2)}) copy-start(f32[512,64]{0,1:T(8,128)} %copy-done.37) | copy-start | bytes 393220
  604.7 26.4 %copy-start.49 = (f32[64]{0:T(128)S(1)}, f32[64]{0:T(128)}, u32[]{:S(2)}) copy-start(f32[64]{0:T(128)} %copy-done.48) | copy-start | bytes 772
  604.8 1.6 collective-permute-start.26
  606.4 7.7 %collective-permute-start.27 = (f32[64,832]{1,0:T(8,128)S(1)}, f32[64,832]{1,0:T(8,128)S(1)}, u32[]{:S(2)}, u32[]{:S(2)}) collective-permute-start(f32[64,832]{1,0:T(8,128)S(1)} %fusion.281), channel_id=1, source_target_pairs={{0,16},{8,24},{16,0},{24,8},{32,48},{40,56},{48,32},{56,40},{64,80... | collective-permute-start | bytes 638984 | tf_op jit(solution)/shard_map/ppermute | solution.py:33
  614.2 8.4 %collective-permute-start.28 = (f32[64,832]{1,0:T(8,128)S(1)}, f32[64,832]{1,0:T(8,128)S(1)}, u32[]{:S(2)}, u32[]{:S(2)}) collective-permute-start(f32[64,832]{1,0:T(8,128)S(1)} %add.360), channel_id=1, source_target_pairs={{0,32},{8,40},{16,48},{24,56},{32,0},{40,8},{48,16},{56,24},{64,96... | collective-permute-start | bytes 638984 | tf_op jit(solution)/shard_map/ppermute | solution.py:33
  622.6 7.6 %collective-permute-start.29 = (f32[64,832]{1,0:T(8,128)S(1)}, f32[64,832]{1,0:T(8,128)S(1)}, u32[]{:S(2)}, u32[]{:S(2)}) collective-permute-start(f32[64,832]{1,0:T(8,128)S(1)} %add.361), channel_id=1, source_target_pairs={{0,64},{8,72},{16,80},{24,88},{32,96},{40,104},{48,112},{56,120},{... | collective-permute-start | bytes 638984 | tf_op jit(solution)/shard_map/ppermute | solution.py:33
  631.7 4.0 collective-permute-start.30
  635.7 4.0 collective-permute-start.31
  639.8 5.4 collective-permute-start.32
  (135 other events, 214.2 us)
where the time goes:
time: 658 us; the launch traced here: 647 us
  matrix products  271 us (41%)
  local copies, waits for them, and re-layouts  142 us (22%)
  waiting for transfers between devices  122 us (19%)
  starting transfers between devices  70.5 us (11%)
  other arithmetic  37.1 us (6%)
    ppermute x23, waiting for transfers between devices, butterfly_sum(): lax.ppermute(value, axis, [(i, i ^ distance) for i in range(count)])  94.9 us
    dot_general x66, matrix products, convolve_blocks(): jnp.einsum('kbm,kmi->kbi', window, matrix, preferred_element_type=jnp.flo...  84.4 us
    while x280, local copies, waits for them, and re-layouts  77.2 us
    dot_general x60, matrix products, correlate_blocks(): jnp.einsum('kbi,kim->kbm', window, matrix, preferred_element_type=jnp.flo...  77 us
    dot_general x6, matrix products, lag_sums(): jnp.dot(grad, band_sums_matrix(block_width, tap_count, offset), precision...  52.1 us
    ppermute x10, starting transfers between devices, passed_along(): lax.ppermute(value, axis, [(source, source + steps) for source in range(l...  42.5 us
    unnamed x70, local copies, waits for them, and re-layouts  32.1 us
    ppermute x23, starting transfers between devices, butterfly_sum(): lax.ppermute(value, axis, [(i, i ^ distance) for i in range(count)])  28 us
  transfers between devices with their start and end apart: 33, of which 31 were waited for; matrix products, arithmetic and copies ran while one was open for 7% of the time, Pallas kernels for 0%

commit v1 on v0

--- a/solution.py
+++ b/solution.py
@@ -6,7 +6,7 @@
 ITERS = 10
 OUTER = 2
 CHUNK = 5
-GHOST_BLOCKS = 10
+GHOST_BLOCKS = 12
 
 
 epsilon = 1e-06
@@ -180,7 +180,9 @@
             wide = both_wide[atoms_all:] if chunk == 0 else widened(latent, ghost)
             wide, _ = lax.fori_loop(0, CHUNK, shrink_step, (wide, wide.astype(jnp.bfloat16)))
             latent = wide[:, ghost : ghost + seg_len]
-        rebuilt, before, latent_b = reconstruct(matrices, latent, block_width, tap_count)
+        before = wide[:, ghost - tap_count : ghost].astype(jnp.bfloat16)
+        latent_b = latent.astype(jnp.bfloat16)
+        rebuilt = convolve_blocks(matrices, latent_b, before, block_width)
         rebuilt_b = rebuilt.astype(jnp.bfloat16)
         row_part = jnp.dot(rebuilt_b, signal.T, preferred_element_type=jnp.float32)
         others = projected - jnp.dot(

time: 658 us -> 741 us (1.13)
  local copies, waits for them, and re-layouts: 142 us -> 225 us
  waiting for transfers between devices: 122 us -> 114 us
    reshape x22, local copies, waits for them, and re-layouts: 7.72 us -> 29.1 us  [convolve_blocks(): jnp.concatenate([before, code_rows], axis=1)]
    reshape x20, local copies, waits for them, and re-layouts: 7.39 us -> 28.7 us  [correlate_blocks(): jnp.concatenate([residual_b, after_rim], axis=1)]
    concatenate x20, local copies, waits for them, and re-layouts: 0.85 us -> 18.2 us  [correlate_blocks(): jnp.concatenate([residual_b, after_rim], axis=1)]
    concatenate x20, local copies, waits for them, and re-layouts: 0.82 us -> 18.2 us  [convolve_blocks(): jnp.concatenate([before, code_rows], axis=1)]
    ppermute x10 -> x8, waiting for transfers between devices: 26.9 us -> 13.6 us  [passed_along(): lax.ppermute(value, axis, [(source, source + steps) for source in range(l...]
    ppermute x10 -> x8, starting transfers between devices: 42.5 us -> 38.1 us  [passed_along(): lax.ppermute(value, axis, [(source, source + steps) for source in range(l...]
  transfers between devices with their start and end apart: 33 -> 31, of which waited for: 31 -> 28; matrix products, arithmetic and copies ran while one was open for 7% -> 6% of each run, Pallas kernels for 0% -> 0%
where the time goes in v1:
time: 741 us; the launch traced here: 727 us
  matrix products  274 us (37%)
  local copies, waits for them, and re-layouts  225 us (30%)
  waiting for transfers between devices  114 us (15%)
  starting transfers between devices  70.4 us (10%)
  other arithmetic  38.8 us (5%)
    ppermute x23, waiting for transfers between devices, butterfly_sum(): lax.ppermute(value, axis, [(i, i ^ distance) for i in range(count)])  101 us
    dot_general x66, matrix products, convolve_blocks(): jnp.einsum('kbm,kmi->kbi', window, matrix, preferred_element_type=jnp.flo...  84.5 us
    while x280, local copies, waits for them, and re-layouts  79.6 us
    dot_general x60, matrix products, correlate_blocks(): jnp.einsum('kbi,kim->kbm', window, matrix, preferred_element_type=jnp.flo...  77.1 us
    dot_general x6, matrix products, lag_sums(): jnp.dot(grad, band_sums_matrix(block_width, tap_count, offset), precision...  52.1 us
    ppermute x8, starting transfers between devices, passed_along(): lax.ppermute(value, axis, [(source, source + steps) for source in range(l...  38.1 us
    ppermute x23, starting transfers between devices, butterfly_sum(): lax.ppermute(value, axis, [(i, i ^ distance) for i in range(count)])  32.4 us
    unnamed x70, local copies, waits for them, and re-layouts  32.1 us
  transfers between devices with their start and end apart: 31, of which 28 were waited for; matrix products, arithmetic and copies ran while one was open for 6% of the time, Pallas kernels for 0%

profile of v1, /device:TPU:4, one launch (start us, length us, event | category | flops | bytes accessed | tf_op | source)
XLA Modules:
  0.0 727.0 jit_solution(12984554318816298094)
XLA Ops:
  7.6 4.5 convolution_convert_fusion.3
  12.1 3.0 collective-permute-start.2
  15.1 2.5 collective-permute-done.2
  20.2 3.5 slice_bitcast_fusion.9
  32.9 8.6 %collective-permute-done.4 = f32[64,2048]{1,0:T(8,128)S(1)} collective-permute-done((f32[64,2048]{1,0:T(8,128)S(1)}, f32[64,2048]{1,0:T(8,128)S(1)}, u32[]{:S(2)}, u32[]{:S(2)}) %collective-permute-start.4) | collective-permute-done | bytes 524320 | tf_op jit(solution)/shard_map/ppermute | solution.py:33
  41.6 4.3 collective-permute-start.5
  57.3 7.7 %collective-permute-start.7 = (f32[128,1536]{1,0:T(8,128)S(1)}, f32[128,1536]{1,0:T(8,128)S(1)}, u32[]{:S(2)}, u32[]{:S(2)}) collective-permute-start(f32[128,1536]{1,0:T(8,128)S(1)} %get-tuple-element.600), channel_id=1, source_target_pairs={{8,0},{16,8},{24,16},{32,24},{40,32},{48,40},{56,48},{64,56},{72,6... | collective-permute-start | bytes 2359304 | tf_op jit(solution)/shard_map/ppermute | solution.py:19
  65.4 7.0 collective-permute-done.6
  76.1 95.9 %while.52 = (s32[]{:T(128)}, f32[64,5120]{1,0:T(8,128)}, bf16[64,5120]{1,0:T(8,128)(2,1)S(1)}, f32[5120]{0:T(1024)S(1)}, f32[64,1]{0,1:T(1,128)S(1)}, /*index=5*...) while((s32[]{:T(128)}, f32[64,5120]{1,0:T(8,128)}, ...), condition=%wide.region_3.4_spmd.clone, body=%wide.region_2.3_spmd.clone.sunk | while | flops 760243200 | bytes 92287848 | solution.py:181
  78.5 2.4 fusion.437
  87.7 2.4 fusion.440
  97.7 2.4 fusion.437
  106.9 2.4 fusion.440
  116.9 2.4 fusion.437
  126.1 2.4 fusion.440
  136.1 2.4 fusion.437
  145.3 2.4 fusion.440
  155.2 2.4 fusion.437
  164.5 2.4 fusion.440
  175.9 7.6 %collective-permute-start.9 = (f32[64,1536]{1,0:T(8,128)S(1)}, f32[64,1536]{1,0:T(8,128)}, u32[]{:S(2)}, u32[]{:S(2)}) collective-permute-start(f32[64,1536]{1,0:T(8,128)S(1)} %get-tuple-element.596), channel_id=1, source_target_pairs={{8,0},{16,8},{24,16},{32,24},{40,32},{48,40},{56,48},{64,56},{72,6... | collective-permute-start | bytes 1179656 | tf_op jit(solution)/shard_map/ppermute | solution.py:19
  192.0 96.1 %while.53 = (s32[]{:T(128)}, f32[64,5120]{1,0:T(8,128)}, bf16[64,5120]{1,0:T(8,128)(2,1)S(1)}, f32[5120]{0:T(1024)S(1)}, f32[64,1]{0,1:T(1,128)S(1)}, /*index=5*...) while((s32[]{:T(128)}, f32[64,5120]{1,0:T(8,128)}, ...), condition=%wide.region_5.6_spmd.clone, body=%wide.region_4.5_spmd.clone.sunk | while | flops 760243200 | bytes 92287848 | solution.py:181
  194.4 2.4 fusion.456
  213.6 2.4 fusion.456
  232.8 2.4 fusion.456
  251.9 2.4 fusion.456
  271.1 2.4 fusion.456
  303.0 7.5 %fusion.131 = f32[64,256]{1,0:T(8,128)S(1)} fusion(f32[64,128,128]{2,1,0:T(8,128)S(1)} %fusion.207), kind=kOutput, calls=%fused_computation.197 | convolution fusion | flops 3233808384 | bytes 4259840 | tf_op jit(solution)/shard_map/dot_general | solution.py:84
  310.5 10.3 %fusion.176 = f32[64,256]{1,0:T(8,128)S(1)} fusion(f32[64,256]{1,0:T(8,128)S(1)} %fusion.131, f32[64,128,128]{2,1,0:T(8,128)S(1)} %fusion.204), kind=kOutput, calls=%fused_computation.206 | convolution fusion | flops 3238019072 | bytes 4325376 | tf_op jit(solution)/shard_map/dot_general | solution.py:84
  320.7 8.3 %fusion.166 = f32[64,256]{1,0:T(8,128)S(1)} fusion(f32[64,256]{1,0:T(8,128)S(1)} %fusion.176, f32[64,128,128]{2,1,0:T(8,128)S(1)} %fusion.201), kind=kOutput, calls=%fused_computation.204 | convolution fusion | flops 3238019072 | bytes 4325376 | tf_op jit(solution)/shard_map/dot_general | solution.py:84
  330.9 7.6 %collective-permute-done.11 = f32[64,832]{1,0:T(8,128)S(1)} collective-permute-done((f32[64,832]{1,0:T(8,128)S(1)}, f32[64,832]{1,0:T(8,128)S(1)}, u32[]{:S(2)}, u32[]{:S(2)}) %collective-permute-start.11) | collective-permute-done | bytes 213024 | tf_op jit(solution)/shard_map/ppermute | solution.py:33
  338.7 8.3 %collective-permute-done.12 = f32[64,832]{1,0:T(8,128)S(1)} collective-permute-done((f32[64,832]{1,0:T(8,128)S(1)}, f32[64,832]{1,0:T(8,128)S(1)}, u32[]{:S(2)}, u32[]{:S(2)}) %collective-permute-start.12) | collective-permute-done | bytes 213024 | tf_op jit(solution)/shard_map/ppermute | solution.py:33
  347.0 3.5 collective-permute-start.13
  350.5 5.0 collective-permute-done.13
  357.7 3.3 collective-permute-done.14
  365.2 2.6 collective-permute-start.16
  368.0 2.6 collective-permute-done.16
  373.2 8.1 %collective-permute-done.17 = f32[64,2048]{1,0:T(8,128)S(1)} collective-permute-done((f32[64,2048]{1,0:T(8,128)S(1)}, f32[64,2048]{1,0:T(8,128)S(1)}, u32[]{:S(2)}, u32[]{:S(2)}) %collective-permute-start.17) | collective-permute-done | bytes 524320 | tf_op jit(solution)/shard_map/ppermute | solution.py:33
  383.9 10.6 %collective-permute-done.18 = f32[64,2048]{1,0:T(8,128)S(1)} collective-permute-done((f32[64,2048]{1,0:T(8,128)S(1)}, f32[64,2048]{1,0:T(8,128)S(1)}, u32[]{:S(2)}, u32[]{:S(2)}) %collective-permute-start.18) | collective-permute-done | bytes 524320 | tf_op jit(solution)/shard_map/ppermute | solution.py:33
  394.5 3.2 collective-permute-start.19
  399.6 5.7 collective-permute-done.19
  407.5 7.7 %collective-permute-start.21 = (f32[128,1536]{1,0:T(8,128)S(1)}, f32[128,1536]{1,0:T(8,128)S(1)}, u32[]{:S(2)}, u32[]{:S(2)}) collective-permute-start(f32[128,1536]{1,0:T(8,128)S(1)} %get-tuple-element.598), channel_id=1, source_target_pairs={{8,0},{16,8},{24,16},{32,24},{40,32},{48,40},{56,48},{64,56},{72,6... | collective-permute-start | bytes 2359304 | tf_op jit(solution)/shard_map/ppermute | solution.py:19
  430.1 95.9 %while.54 = (s32[]{:T(128)}, f32[64,5120]{1,0:T(8,128)}, bf16[64,5120]{1,0:T(8,128)(2,1)S(1)}, f32[5120]{0:T(1024)S(1)}, f32[64,1]{0,1:T(1,128)S(1)}, /*index=5*...) while((s32[]{:T(128)}, f32[64,5120]{1,0:T(8,128)}, ...), condition=%wide.region_8.9_spmd.clone, body=%wide.region_7.8_spmd.clone.sunk | while | flops 760243200 | bytes 92287848 | solution.py:181
  432.4 2.4 fusion.475
  451.6 2.4 fusion.475
  470.8 2.4 fusion.475
  490.0 2.4 fusion.475
  509.2 2.4 fusion.475
  529.8 7.4 %collective-permute-start.23 = (f32[64,1536]{1,0:T(8,128)S(1)}, f32[64,1536]{1,0:T(8,128)}, u32[]{:S(2)}, u32[]{:S(2)}) collective-permute-start(f32[64,1536]{1,0:T(8,128)S(1)} %get-tuple-element.594), channel_id=1, source_target_pairs={{8,0},{16,8},{24,16},{32,24},{40,32},{48,40},{56,48},{64,56},{72,6... | collective-permute-start | bytes 1179656 | tf_op jit(solution)/shard_map/ppermute | solution.py:19
  545.8 96.1 %while.55 = (s32[]{:T(128)}, f32[64,5120]{1,0:T(8,128)}, bf16[64,5120]{1,0:T(8,128)(2,1)S(1)}, f32[5120]{0:T(1024)S(1)}, f32[64,1]{0,1:T(1,128)S(1)}, /*index=5*...) while((s32[]{:T(128)}, f32[64,5120]{1,0:T(8,128)}, ...), condition=%wide.region_10.11_spmd.clone, body=%wide.region_9.10_spmd.clone.sunk | while | flops 760243200 | bytes 92287848 | solution.py:181
  548.2 2.4 fusion.494
  567.3 2.4 fusion.494
  586.5 2.4 fusion.494
  605.7 2.4 fusion.494
  624.9 2.4 fusion.494
  657.6 7.5 %fusion.136 = f32[64,256]{1,0:T(8,128)S(1)} fusion(f32[64,128,128]{2,1,0:T(8,128)S(1)} %fusion.197), kind=kOutput, calls=%fused_computation.198 | convolution fusion | flops 3233808384 | bytes 4259840 | tf_op jit(solution)/shard_map/dot_general | solution.py:84
  665.0 10.3 %fusion.171 = f32[64,256]{1,0:T(8,128)S(1)} fusion(f32[64,256]{1,0:T(8,128)S(1)} %fusion.136, f32[64,128,128]{2,1,0:T(8,128)S(1)} %fusion.194), kind=kOutput, calls=%fused_computation.205 | convolution fusion | flops 3238019072 | bytes 4325376 | tf_op jit(solution)/shard_map/dot_general | solution.py:84
  675.3 8.3 %fusion.161 = f32[64,256]{1,0:T(8,128)S(1)} fusion(f32[64,256]{1,0:T(8,128)S(1)} %fusion.171, f32[64,128,128]{2,1,0:T(8,128)S(1)} %fusion.191), kind=kOutput, calls=%fused_computation.203 | convolution fusion | flops 3238019072 | bytes 4325376 | tf_op jit(solution)/shard_map/dot_general | solution.py:84
  685.5 7.6 %collective-permute-done.25 = f32[64,832]{1,0:T(8,128)S(1)} collective-permute-done((f32[64,832]{1,0:T(8,128)S(1)}, f32[64,832]{1,0:T(8,128)S(1)}, u32[]{:S(2)}, u32[]{:S(2)}) %collective-permute-start.25) | collective-permute-done | bytes 213024 | tf_op jit(solution)/shard_map/ppermute | solution.py:33
  693.2 8.3 %collective-permute-done.26 = f32[64,832]{1,0:T(8,128)S(1)} collective-permute-done((f32[64,832]{1,0:T(8,128)S(1)}, f32[64,832]{1,0:T(8,128)S(1)}, u32[]{:S(2)}, u32[]{:S(2)}) %collective-permute-start.26) | collective-permute-done | bytes 213024 | tf_op jit(solution)/shard_map/ppermute | solution.py:33
  701.6 3.5 collective-permute-start.27
  705.1 5.0 collective-permute-done.27
  712.7 2.9 collective-permute-done.28
  715.6 4.2 collective-permute-done.29
  719.8 2.9 collective-permute-start.30
  (730 shorter events, 451.4 us)
Async XLA Ops:
  0.6 17.8 %copy-start = (bf16[512,2048]{1,0:T(8,128)(2,1)S(1)}, bf16[512,2048]{1,0:T(8,128)(2,1)}, u32[]{:S(2)}) copy-start(bf16[512,2048]{1,0:T(8,128)(2,1)} %param.15) | copy-start | bytes 6291460
  2.0 4.0 collective-permute-start
  3.3 8.8 %copy-start.44 = (s32[16384]{0:T(1024)}, s32[16384]{0:T(1024)S(1)}, u32[]{:S(2)}) copy-start(s32[16384]{0:T(1024)S(1)} %add_bitcast_fusion.1) | copy-start | bytes 196612
  6.0 6.1 collective-permute-start.1
  7.6 10.8 %copy-start.37 = (f32[512,64]{0,1:T(8,128)S(1)}, f32[512,64]{0,1:T(8,128)}, u32[]{:S(2)}) copy-start(f32[512,64]{0,1:T(8,128)} %param.16) | copy-start | bytes 393220
  12.1 5.5 collective-permute-start.2
  18.4 46.9 %copy-start.50 = (f32[64]{0:T(128)}, f32[64]{0:T(128)S(1)}, u32[]{:S(2)}) copy-start(f32[64]{0:T(128)S(1)} %add_rsqrt_fusion.2) | copy-start | bytes 772
  19.0 11.5 %collective-permute-start.3 = (f32[64,2048]{1,0:T(8,128)S(1)}, f32[64,2048]{1,0:T(8,128)S(1)}, u32[]{:S(2)}, u32[]{:S(2)}) collective-permute-start(f32[64,2048]{1,0:T(8,128)S(1)} %fusion.221), channel_id=1, source_target_pairs={{0,1},{1,0},{2,3},{3,2},{4,5},{5,4},{6,7},{7,6},{8,9},{9,8},{10,11... | collective-permute-start | bytes 1572872 | tf_op jit(solution)/shard_map/ppermute | solution.py:33
  29.4 3.4 copy-start.46
  30.5 11.0 %collective-permute-start.4 = (f32[64,2048]{1,0:T(8,128)S(1)}, f32[64,2048]{1,0:T(8,128)S(1)}, u32[]{:S(2)}, u32[]{:S(2)}) collective-permute-start(f32[64,2048]{1,0:T(8,128)S(1)} %add.325), channel_id=1, source_target_pairs={{0,2},{1,3},{2,0},{3,1},{4,6},{5,7},{6,4},{7,5},{8,10},{9,11},{10,... | collective-permute-start | bytes 1572872 | tf_op jit(solution)/shard_map/ppermute | solution.py:33
  41.6 4.9 copy-start.36
  41.6 12.4 %collective-permute-start.5 = (f32[64,2048]{1,0:T(8,128)S(1)}, f32[64,2048]{1,0:T(8,128)}, u32[]{:S(2)}, u32[]{:S(2)}) collective-permute-start(f32[64,2048]{1,0:T(8,128)S(1)} %add.326), channel_id=1, source_target_pairs={{0,4},{1,5},{2,6},{3,7},{4,0},{5,1},{6,2},{7,3},{8,12},{9,13},{10,... | collective-permute-start | bytes 1572872 | tf_op jit(solution)/shard_map/ppermute | solution.py:33
  50.4 4.9 copy-start.35
  52.3 12.7 %copy-start.52 = (s32[16]{0:T(128)S(1)}, s32[16]{0:T(128)}, u32[]{:S(2)}) copy-start(s32[16]{0:T(128)} %param.21) | copy-start | bytes 196
  52.4 12.9 %copy-start.43 = (f32[64]{0:T(128)S(1)}, f32[64]{0:T(128)}, u32[]{:S(2)}) copy-start(f32[64]{0:T(128)} %param.20) | copy-start | bytes 772
  52.4 12.9 %copy-start.53 = (f32[64]{0:T(128)S(1)}, f32[64]{0:T(128)}, u32[]{:S(2)}) copy-start(f32[64]{0:T(128)} %param.19) | copy-start | bytes 772
  55.4 16.9 %collective-permute-start.6 = (f32[128,1536]{1,0:T(8,128)S(1)}, f32[128,1536]{1,0:T(8,128)S(1)}, u32[]{:S(2)}, u32[]{:S(2)}) collective-permute-start(f32[128,1536]{1,0:T(8,128)S(1)} %get-tuple-element.599), channel_id=1, source_target_pairs={{0,8},{8,16},{16,24},{24,32},{32,40},{40,48},{48,56},{56,64},{64,7... | collective-permute-start | bytes 2359304 | tf_op jit(solution)/shard_map/ppermute | solution.py:19
  57.3 16.8 %collective-permute-start.7 = (f32[128,1536]{1,0:T(8,128)S(1)}, f32[128,1536]{1,0:T(8,128)S(1)}, u32[]{:S(2)}, u32[]{:S(2)}) collective-permute-start(f32[128,1536]{1,0:T(8,128)S(1)} %get-tuple-element.600), channel_id=1, source_target_pairs={{8,0},{16,8},{24,16},{32,24},{40,32},{48,40},{56,48},{64,56},{72,6... | collective-permute-start | bytes 2359304 | tf_op jit(solution)/shard_map/ppermute | solution.py:19
  78.5 2.4 copy-start.1
  97.7 2.4 copy-start.1
  116.9 2.4 copy-start.1
  136.0 2.4 copy-start.1
  155.2 2.4 copy-start.1
  174.0 13.1 %collective-permute-start.8 = (f32[64,1536]{1,0:T(8,128)}, f32[64,1536]{1,0:T(8,128)S(1)}, u32[]{:S(2)}, u32[]{:S(2)}) collective-permute-start(f32[64,1536]{1,0:T(8,128)} %get-tuple-element.595), channel_id=1, source_target_pairs={{0,8},{8,16},{16,24},{24,32},{32,40},{40,48},{48,56},{56,64},{64,7... | collective-permute-start | bytes 1179656 | tf_op jit(solution)/shard_map/ppermute | solution.py:19
  175.9 12.7 %collective-permute-start.9 = (f32[64,1536]{1,0:T(8,128)S(1)}, f32[64,1536]{1,0:T(8,128)}, u32[]{:S(2)}, u32[]{:S(2)}) collective-permute-start(f32[64,1536]{1,0:T(8,128)S(1)} %get-tuple-element.596), channel_id=1, source_target_pairs={{8,0},{16,8},{24,16},{32,24},{40,32},{48,40},{56,48},{64,56},{72,6... | collective-permute-start | bytes 1179656 | tf_op jit(solution)/shard_map/ppermute | solution.py:19
  194.4 2.4 copy-start.2
  213.6 2.4 copy-start.2
  232.8 2.4 copy-start.2
  251.9 2.4 copy-start.2
  271.1 2.4 copy-start.2
  329.0 27.3 %copy-start.38 = (f32[512,64]{0,1:T(8,128)S(1)}, f32[512,64]{0,1:T(8,128)}, u32[]{:S(2)}) copy-start(f32[512,64]{0,1:T(8,128)} %param.16) | copy-start | bytes 393220
  329.0 27.3 %copy-start.51 = (f32[64]{0:T(128)S(1)}, f32[64]{0:T(128)}, u32[]{:S(2)}) copy-start(f32[64]{0:T(128)} %copy-done.50) | copy-start | bytes 772
  329.1 1.6 collective-permute-start.10
  330.8 7.7 %collective-permute-start.11 = (f32[64,832]{1,0:T(8,128)S(1)}, f32[64,832]{1,0:T(8,128)S(1)}, u32[]{:S(2)}, u32[]{:S(2)}) collective-permute-start(f32[64,832]{1,0:T(8,128)S(1)} %fusion.282), channel_id=1, source_target_pairs={{0,16},{8,24},{16,0},{24,8},{32,48},{40,56},{48,32},{56,40},{64,80... | collective-permute-start | bytes 638984 | tf_op jit(solution)/shard_map/ppermute | solution.py:33
  338.6 8.4 %collective-permute-start.12 = (f32[64,832]{1,0:T(8,128)S(1)}, f32[64,832]{1,0:T(8,128)S(1)}, u32[]{:S(2)}, u32[]{:S(2)}) collective-permute-start(f32[64,832]{1,0:T(8,128)S(1)} %add.344), channel_id=1, source_target_pairs={{0,32},{8,40},{16,48},{24,56},{32,0},{40,8},{48,16},{56,24},{64,96... | collective-permute-start | bytes 638984 | tf_op jit(solution)/shard_map/ppermute | solution.py:33
  347.0 8.5 %collective-permute-start.13 = (f32[64,832]{1,0:T(8,128)S(1)}, f32[64,832]{1,0:T(8,128)S(1)}, u32[]{:S(2)}, u32[]{:S(2)}) collective-permute-start(f32[64,832]{1,0:T(8,128)S(1)} %add.345), channel_id=1, source_target_pairs={{0,64},{8,72},{16,80},{24,88},{32,96},{40,104},{48,112},{56,120},{... | collective-permute-start | bytes 638984 | tf_op jit(solution)/shard_map/ppermute | solution.py:33
  356.7 15.2 %copy-start.33 = (f32[512,64]{0,1:T(8,128)}, f32[512,64]{0,1:T(8,128)S(1)}, u32[]{:S(2)}) copy-start(f32[512,64]{0,1:T(8,128)S(1)} %fusion.212) | copy-start | bytes 393220
  357.0 4.0 collective-permute-start.14
  361.0 4.2 collective-permute-start.15
  365.2 5.4 collective-permute-start.16
  371.4 56.5 %copy-start.48 = (f32[64]{0:T(128)}, f32[64]{0:T(128)S(1)}, u32[]{:S(2)}) copy-start(f32[64]{0:T(128)S(1)} %add_rsqrt_fusion.1) | copy-start | bytes 772
  371.4 10.6 %copy-start.47 = (s32[16384]{0:T(1024)S(1)}, s32[16384]{0:T(1024)}, u32[]{:S(2)}) copy-start(s32[16384]{0:T(1024)} %copy-done.46) | copy-start | bytes 196612
  372.0 9.3 %collective-permute-start.17 = (f32[64,2048]{1,0:T(8,128)S(1)}, f32[64,2048]{1,0:T(8,128)S(1)}, u32[]{:S(2)}, u32[]{:S(2)}) collective-permute-start(f32[64,2048]{1,0:T(8,128)S(1)} %fusion.222), channel_id=1, source_target_pairs={{0,1},{1,0},{2,3},{3,2},{4,5},{5,4},{6,7},{7,6},{8,9},{9,8},{10,11... | collective-permute-start | bytes 1572872 | tf_op jit(solution)/shard_map/ppermute | solution.py:33
  381.3 13.2 %collective-permute-start.18 = (f32[64,2048]{1,0:T(8,128)S(1)}, f32[64,2048]{1,0:T(8,128)S(1)}, u32[]{:S(2)}, u32[]{:S(2)}) collective-permute-start(f32[64,2048]{1,0:T(8,128)S(1)} %add.351), channel_id=1, source_target_pairs={{0,2},{1,3},{2,0},{3,1},{4,6},{5,7},{6,4},{7,5},{8,10},{9,11},{10,... | collective-permute-start | bytes 1572872 | tf_op jit(solution)/shard_map/ppermute | solution.py:33
  382.0 15.7 %copy-start.45 = (s32[16384]{0:T(1024)S(1)}, s32[16384]{0:T(1024)}, u32[]{:S(2)}) copy-start(s32[16384]{0:T(1024)} %copy-done.44) | copy-start | bytes 196612
  394.5 10.8 %collective-permute-start.19 = (f32[64,2048]{1,0:T(8,128)S(1)}, f32[64,2048]{1,0:T(8,128)S(1)}, u32[]{:S(2)}, u32[]{:S(2)}) collective-permute-start(f32[64,2048]{1,0:T(8,128)S(1)} %add.352), channel_id=1, source_target_pairs={{0,4},{1,5},{2,6},{3,7},{4,0},{5,1},{6,2},{7,3},{8,12},{9,13},{10,... | collective-permute-start | bytes 1572872 | tf_op jit(solution)/shard_map/ppermute | solution.py:33
  405.5 22.5 %collective-permute-start.20 = (f32[128,1536]{1,0:T(8,128)S(1)}, f32[128,1536]{1,0:T(8,128)S(1)}, u32[]{:S(2)}, u32[]{:S(2)}) collective-permute-start(f32[128,1536]{1,0:T(8,128)S(1)} %get-tuple-element.597), channel_id=1, source_target_pairs={{0,8},{8,16},{16,24},{24,32},{32,40},{40,48},{48,56},{56,64},{64,7... | collective-permute-start | bytes 2359304 | tf_op jit(solution)/shard_map/ppermute | solution.py:19
  407.5 20.6 %collective-permute-start.21 = (f32[128,1536]{1,0:T(8,128)S(1)}, f32[128,1536]{1,0:T(8,128)S(1)}, u32[]{:S(2)}, u32[]{:S(2)}) collective-permute-start(f32[128,1536]{1,0:T(8,128)S(1)} %get-tuple-element.598), channel_id=1, source_target_pairs={{8,0},{16,8},{24,16},{32,24},{40,32},{48,40},{56,48},{64,56},{72,6... | collective-permute-start | bytes 2359304 | tf_op jit(solution)/shard_map/ppermute | solution.py:19
  432.4 2.4 copy-start.7
  451.6 2.4 copy-start.7
  470.8 2.4 copy-start.7
  490.0 2.4 copy-start.7
  509.2 2.4 copy-start.7
  527.9 12.9 %collective-permute-start.22 = (f32[64,1536]{1,0:T(8,128)}, f32[64,1536]{1,0:T(8,128)S(1)}, u32[]{:S(2)}, u32[]{:S(2)}) collective-permute-start(f32[64,1536]{1,0:T(8,128)} %get-tuple-element.593), channel_id=1, source_target_pairs={{0,8},{8,16},{16,24},{24,32},{32,40},{40,48},{48,56},{56,64},{64,7... | collective-permute-start | bytes 1179656 | tf_op jit(solution)/shard_map/ppermute | solution.py:19
  529.8 12.5 %collective-permute-start.23 = (f32[64,1536]{1,0:T(8,128)S(1)}, f32[64,1536]{1,0:T(8,128)}, u32[]{:S(2)}, u32[]{:S(2)}) collective-permute-start(f32[64,1536]{1,0:T(8,128)S(1)} %get-tuple-element.594), channel_id=1, source_target_pairs={{8,0},{16,8},{24,16},{32,24},{40,32},{48,40},{56,48},{64,56},{72,6... | collective-permute-start | bytes 1179656 | tf_op jit(solution)/shard_map/ppermute | solution.py:19
  683.6 27.3 %copy-start.34 = (f32[512,64]{0,1:T(8,128)S(1)}, f32[512,64]{0,1:T(8,128)}, u32[]{:S(2)}) copy-start(f32[512,64]{0,1:T(8,128)} %copy-done.33) | copy-start | bytes 393220
  683.6 27.3 %copy-start.49 = (f32[64]{0:T(128)S(1)}, f32[64]{0:T(128)}, u32[]{:S(2)}) copy-start(f32[64]{0:T(128)} %copy-done.48) | copy-start | bytes 772
  683.7 1.6 collective-permute-start.24
  685.4 7.7 %collective-permute-start.25 = (f32[64,832]{1,0:T(8,128)S(1)}, f32[64,832]{1,0:T(8,128)S(1)}, u32[]{:S(2)}, u32[]{:S(2)}) collective-permute-start(f32[64,832]{1,0:T(8,128)S(1)} %fusion.281), channel_id=1, source_target_pairs={{0,16},{8,24},{16,0},{24,8},{32,48},{40,56},{48,32},{56,40},{64,80... | collective-permute-start | bytes 638984 | tf_op jit(solution)/shard_map/ppermute | solution.py:33
  693.1 8.4 %collective-permute-start.26 = (f32[64,832]{1,0:T(8,128)S(1)}, f32[64,832]{1,0:T(8,128)S(1)}, u32[]{:S(2)}, u32[]{:S(2)}) collective-permute-start(f32[64,832]{1,0:T(8,128)S(1)} %add.360), channel_id=1, source_target_pairs={{0,32},{8,40},{16,48},{24,56},{32,0},{40,8},{48,16},{56,24},{64,96... | collective-permute-start | bytes 638984 | tf_op jit(solution)/shard_map/ppermute | solution.py:33
  701.6 8.5 %collective-permute-start.27 = (f32[64,832]{1,0:T(8,128)S(1)}, f32[64,832]{1,0:T(8,128)S(1)}, u32[]{:S(2)}, u32[]{:S(2)}) collective-permute-start(f32[64,832]{1,0:T(8,128)S(1)} %add.361), channel_id=1, source_target_pairs={{0,64},{8,72},{16,80},{24,88},{32,96},{40,104},{48,112},{56,120},{... | collective-permute-start | bytes 638984 | tf_op jit(solution)/shard_map/ppermute | solution.py:33
  711.6 4.0 collective-permute-start.28
  715.6 4.2 collective-permute-start.29
  719.8 5.4 collective-permute-start.30
  (133 other events, 211.2 us)

commit v2 on v0

--- a/solution.py
+++ b/solution.py
@@ -34,6 +34,11 @@
         value = value + partner
         distance *= 2
     return value
+
+
+def dense_sum(square, axis):
+    rows, cols = square.shape
+    return butterfly_sum(square.reshape(rows * cols // 128, 128), axis).reshape(rows, cols)
 
 
 def one_hot_skew(block_width, tap_span, transposed=False):
@@ -138,7 +143,7 @@
     ).astype(jnp.float32)
     allowed_wide = inside * jnp.where(jnp.any(wide_crosses, axis=0), 0.0, 1.0).astype(jnp.float32)
     zero_rim = jnp.zeros((atoms_all, tap_count), jnp.bfloat16)
-    raw_start = butterfly_sum(jnp.dot(spatial.T, spatial, precision=highest), "chan")
+    raw_start = dense_sum(jnp.dot(spatial.T, spatial, precision=highest), "chan")
     scaling = 1.0 / jnp.sqrt(jnp.diag(raw_start) + epsilon)
     space_loc = spatial * scaling[None, :]
     gram_matrix = raw_start * scaling[:, None] * scaling[None, :]
@@ -196,7 +201,7 @@
         raw_rows = stats_rows - jnp.dot(
             space_loc, cross_gram - jnp.diag(jnp.diag(cross_gram)), precision=highest
         )
-        raw_gram = butterfly_sum(jnp.dot(raw_rows.T, raw_rows, precision=highest), "chan")
+        raw_gram = dense_sum(jnp.dot(raw_rows.T, raw_rows, precision=highest), "chan")
         scaling = 1.0 / jnp.sqrt(jnp.diag(raw_gram) + epsilon)
         space_loc = raw_rows * scaling[None, :]
         gram_matrix = raw_gram * scaling[:, None] * scaling[None, :]

time: 658 us -> 660 us (level)
  transfers between devices with their start and end apart: 33 -> 33, of which waited for: 31 -> 30; matrix products, arithmetic and copies ran while one was open for 7% -> 8% of each run, Pallas kernels for 0% -> 0%
where the time goes in v2:
time: 660 us; the launch traced here: 649 us
  matrix products  271 us (41%)
  local copies, waits for them, and re-layouts  146 us (22%)
  waiting for transfers between devices  121 us (18%)
  starting transfers between devices  66.8 us (10%)
  other arithmetic  39.9 us (6%)
    ppermute x23, waiting for transfers between devices, butterfly_sum(): lax.ppermute(value, axis, [(i, i ^ distance) for i in range(count)])  97.5 us
    dot_general x66, matrix products, convolve_blocks(): jnp.einsum('kbm,kmi->kbi', window, matrix, preferred_element_type=jnp.flo...  84.4 us
    while x280, local copies, waits for them, and re-layouts  77 us
    dot_general x60, matrix products, correlate_blocks(): jnp.einsum('kbi,kim->kbm', window, matrix, preferred_element_type=jnp.flo...  77 us
    dot_general x6, matrix products, lag_sums(): jnp.dot(grad, band_sums_matrix(block_width, tap_count, offset), precision...  52 us
    ppermute x10, starting transfers between devices, passed_along(): lax.ppermute(value, axis, [(source, source + steps) for source in range(l...  42.5 us
    unnamed x70, local copies, waits for them, and re-layouts  32.9 us
    dot_general x20, matrix products, mix_atoms(): return jnp.dot(own_gram, rebuilt_part, precision=highest)  27.7 us
  transfers between devices with their start and end apart: 33, of which 30 were waited for; matrix products, arithmetic and copies ran while one was open for 8% of the time, Pallas kernels for 0%

profile of v2, /device:TPU:4, one launch (start us, length us, event | category | flops | bytes accessed | tf_op | source)
XLA Modules:
  0.0 649.1 jit_solution(7044973216137342969)
XLA Ops:
  7.4 4.5 convolution_convert_fusion.3
  11.9 3.0 collective-permute-start.2
  19.9 3.5 slice_bitcast_fusion.9
  32.8 8.6 %collective-permute-done.4 = f32[64,2048]{1,0:T(8,128)S(1)} collective-permute-done((f32[64,2048]{1,0:T(8,128)S(1)}, f32[64,2048]{1,0:T(8,128)S(1)}, u32[]{:S(2)}, u32[]{:S(2)}) %collective-permute-start.4) | collective-permute-done | bytes 524320 | tf_op jit(solution)/shard_map/ppermute | solution.py:33
  41.4 4.3 collective-permute-start.5
  58.4 7.7 %collective-permute-start.7 = (f32[128,1280]{1,0:T(8,128)S(1)}, f32[128,1280]{1,0:T(8,128)S(1)}, u32[]{:S(2)}, u32[]{:S(2)}) collective-permute-start(f32[128,1280]{1,0:T(8,128)S(1)} %get-tuple-element.602), channel_id=1, source_target_pairs={{8,0},{16,8},{24,16},{32,24},{40,32},{48,40},{56,48},{64,56},{72,6... | collective-permute-start | bytes 1966088 | tf_op jit(solution)/shard_map/ppermute | solution.py:19
  66.3 5.7 collective-permute-done.6
  76.7 74.7 %while.52 = (s32[]{:T(128)}, f32[64,4608]{1,0:T(8,128)}, bf16[64,4608]{1,0:T(8,128)(2,1)S(1)}, f32[4608]{0:T(1024)S(1)}, f32[64,1]{0,1:T(1,128)S(1)}, /*index=5*...) while((s32[]{:T(128)}, f32[64,4608]{1,0:T(8,128)}, ...), condition=%wide.region_3.4_spmd.clone, body=%wide.region_2.3_spmd.clone.sunk | while | flops 684218880 | bytes 87890792 | solution.py:186
  77.2 2.4 fusion.429
  92.1 2.4 fusion.429
  99.2 2.4 fusion.432
  107.0 2.4 fusion.429
  121.9 2.4 fusion.429
  129.1 2.4 fusion.432
  136.9 2.4 fusion.429
  155.1 7.6 %collective-permute-start.9 = (f32[64,1280]{1,0:T(8,128)S(1)}, f32[64,1280]{1,0:T(8,128)}, u32[]{:S(2)}, u32[]{:S(2)}) collective-permute-start(f32[64,1280]{1,0:T(8,128)S(1)} %get-tuple-element.598), channel_id=1, source_target_pairs={{8,0},{16,8},{24,16},{32,24},{40,32},{48,40},{56,48},{64,56},{72,6... | collective-permute-start | bytes 983048 | tf_op jit(solution)/shard_map/ppermute | solution.py:19
  170.5 74.6 %while.53 = (s32[]{:T(128)}, f32[64,4608]{1,0:T(8,128)}, bf16[64,4608]{1,0:T(8,128)(2,1)S(1)}, f32[4608]{0:T(1024)S(1)}, f32[64,1]{0,1:T(1,128)S(1)}, /*index=5*...) while((s32[]{:T(128)}, f32[64,4608]{1,0:T(8,128)}, ...), condition=%wide.region_5.6_spmd.clone, body=%wide.region_4.5_spmd.clone.sunk | while | flops 684218880 | bytes 87890792 | solution.py:186
  170.9 2.4 fusion.448
  185.9 2.4 fusion.448
  193.0 2.4 fusion.451
  200.8 2.4 fusion.448
  215.7 2.4 fusion.448
  222.8 2.4 fusion.451
  230.6 2.4 fusion.448
  249.0 6.3 collective-permute-done.10
  268.6 7.5 %fusion.131 = f32[64,256]{1,0:T(8,128)S(1)} fusion(f32[64,128,128]{2,1,0:T(8,128)S(1)} %fusion.208), kind=kOutput, calls=%fused_computation.197 | convolution fusion | flops 3233808384 | bytes 4259840 | tf_op jit(solution)/shard_map/dot_general | solution.py:89
  276.1 10.3 %fusion.176 = f32[64,256]{1,0:T(8,128)S(1)} fusion(f32[64,256]{1,0:T(8,128)S(1)} %fusion.131, f32[64,128,128]{2,1,0:T(8,128)S(1)} %fusion.204), kind=kOutput, calls=%fused_computation.206 | convolution fusion | flops 3238019072 | bytes 4325376 | tf_op jit(solution)/shard_map/dot_general | solution.py:89
  286.4 8.3 %fusion.166 = f32[64,256]{1,0:T(8,128)S(1)} fusion(f32[64,256]{1,0:T(8,128)S(1)} %fusion.176, f32[64,128,128]{2,1,0:T(8,128)S(1)} %fusion.201), kind=kOutput, calls=%fused_computation.204 | convolution fusion | flops 3238019072 | bytes 4325376 | tf_op jit(solution)/shard_map/dot_general | solution.py:89
  296.5 7.6 %collective-permute-done.12 = f32[64,832]{1,0:T(8,128)S(1)} collective-permute-done((f32[64,832]{1,0:T(8,128)S(1)}, f32[64,832]{1,0:T(8,128)S(1)}, u32[]{:S(2)}, u32[]{:S(2)}) %collective-permute-start.12) | collective-permute-done | bytes 213024 | tf_op jit(solution)/shard_map/ppermute | solution.py:33
  304.3 8.3 %collective-permute-done.13 = f32[64,832]{1,0:T(8,128)S(1)} collective-permute-done((f32[64,832]{1,0:T(8,128)S(1)}, f32[64,832]{1,0:T(8,128)S(1)}, u32[]{:S(2)}, u32[]{:S(2)}) %collective-permute-start.13) | collective-permute-done | bytes 213024 | tf_op jit(solution)/shard_map/ppermute | solution.py:33
  312.7 7.5 %collective-permute-done.14 = f32[64,832]{1,0:T(8,128)S(1)} collective-permute-done((f32[64,832]{1,0:T(8,128)S(1)}, f32[64,832]{1,0:T(8,128)S(1)}, u32[]{:S(2)}, u32[]{:S(2)}) %collective-permute-start.14) | collective-permute-done | bytes 213024 | tf_op jit(solution)/shard_map/ppermute | solution.py:33
  322.3 3.3 collective-permute-done.15
  329.5 2.5 collective-permute-start.17
  332.2 2.5 collective-permute-done.17
  337.8 7.6 %collective-permute-done.18 = f32[64,2048]{1,0:T(8,128)S(1)} collective-permute-done((f32[64,2048]{1,0:T(8,128)S(1)}, f32[64,2048]{1,0:T(8,128)S(1)}, u32[]{:S(2)}, u32[]{:S(2)}) %collective-permute-start.18) | collective-permute-done | bytes 524320 | tf_op jit(solution)/shard_map/ppermute | solution.py:33
  354.7 3.9 collective-permute-done.19
  358.6 2.9 collective-permute-start.20
  363.4 6.0 collective-permute-done.20
  371.5 7.7 %collective-permute-start.22 = (f32[128,1280]{1,0:T(8,128)S(1)}, f32[128,1280]{1,0:T(8,128)S(1)}, u32[]{:S(2)}, u32[]{:S(2)}) collective-permute-start(f32[128,1280]{1,0:T(8,128)S(1)} %get-tuple-element.600), channel_id=1, source_target_pairs={{8,0},{16,8},{24,16},{32,24},{40,32},{48,40},{56,48},{64,56},{72,6... | collective-permute-start | bytes 1966088 | tf_op jit(solution)/shard_map/ppermute | solution.py:19
  388.7 74.6 %while.54 = (s32[]{:T(128)}, f32[64,4608]{1,0:T(8,128)}, bf16[64,4608]{1,0:T(8,128)(2,1)S(1)}, f32[4608]{0:T(1024)S(1)}, f32[64,1]{0,1:T(1,128)S(1)}, /*index=5*...) while((s32[]{:T(128)}, f32[64,4608]{1,0:T(8,128)}, ...), condition=%wide.region_8.9_spmd.clone, body=%wide.region_7.8_spmd.clone.sunk | while | flops 684218880 | bytes 87890792 | solution.py:186
  389.1 2.4 fusion.467
  404.1 2.4 fusion.467
  419.0 2.4 fusion.467
  433.9 2.4 fusion.467
  448.8 2.4 fusion.467
  456.0 2.4 fusion.470
  467.1 7.6 %collective-permute-start.24 = (f32[64,1280]{1,0:T(8,128)S(1)}, f32[64,1280]{1,0:T(8,128)}, u32[]{:S(2)}, u32[]{:S(2)}) collective-permute-start(f32[64,1280]{1,0:T(8,128)S(1)} %get-tuple-element.596), channel_id=1, source_target_pairs={{8,0},{16,8},{24,16},{32,24},{40,32},{48,40},{56,48},{64,56},{72,6... | collective-permute-start | bytes 983048 | tf_op jit(solution)/shard_map/ppermute | solution.py:19
  482.4 74.6 %while.55 = (s32[]{:T(128)}, f32[64,4608]{1,0:T(8,128)}, bf16[64,4608]{1,0:T(8,128)(2,1)S(1)}, f32[4608]{0:T(1024)S(1)}, f32[64,1]{0,1:T(1,128)S(1)}, /*index=5*...) while((s32[]{:T(128)}, f32[64,4608]{1,0:T(8,128)}, ...), condition=%wide.region_10.11_spmd.clone, body=%wide.region_9.10_spmd.clone.sunk | while | flops 684218880 | bytes 87890792 | solution.py:186
  482.9 2.4 fusion.486
  497.8 2.4 fusion.486
  504.9 2.4 fusion.489
  512.7 2.4 fusion.486
  527.6 2.4 fusion.486
  542.6 2.4 fusion.486
  561.2 6.9 %collective-permute-done.25 = bf16[64,256]{1,0:T(8,128)(2,1)S(1)} collective-permute-done((bf16[64,256]{1,0:T(8,128)(2,1)S(1)}, bf16[64,256]{1,0:T(8,128)(2,1)S(1)}, u32[]{:S(2)}, u32[]{:S(2)}) %collective-permute-start.25) | collective-permute-done | bytes 32800 | tf_op jit(solution)/shard_map/ppermute | solution.py:19
  581.4 7.5 %fusion.136 = f32[64,256]{1,0:T(8,128)S(1)} fusion(f32[64,128,128]{2,1,0:T(8,128)S(1)} %fusion.198), kind=kOutput, calls=%fused_computation.198 | convolution fusion | flops 3233808384 | bytes 4259840 | tf_op jit(solution)/shard_map/dot_general | solution.py:89
  588.8 10.3 %fusion.171 = f32[64,256]{1,0:T(8,128)S(1)} fusion(f32[64,256]{1,0:T(8,128)S(1)} %fusion.136, f32[64,128,128]{2,1,0:T(8,128)S(1)} %fusion.194), kind=kOutput, calls=%fused_computation.205 | convolution fusion | flops 3238019072 | bytes 4325376 | tf_op jit(solution)/shard_map/dot_general | solution.py:89
  599.1 8.3 %fusion.161 = f32[64,256]{1,0:T(8,128)S(1)} fusion(f32[64,256]{1,0:T(8,128)S(1)} %fusion.171, f32[64,128,128]{2,1,0:T(8,128)S(1)} %fusion.191), kind=kOutput, calls=%fused_computation.203 | convolution fusion | flops 3238019072 | bytes 4325376 | tf_op jit(solution)/shard_map/dot_general | solution.py:89
  609.3 7.6 %collective-permute-done.27 = f32[64,832]{1,0:T(8,128)S(1)} collective-permute-done((f32[64,832]{1,0:T(8,128)S(1)}, f32[64,832]{1,0:T(8,128)S(1)}, u32[]{:S(2)}, u32[]{:S(2)}) %collective-permute-start.27) | collective-permute-done | bytes 213024 | tf_op jit(solution)/shard_map/ppermute | solution.py:33
  617.0 8.3 %collective-permute-done.28 = f32[64,832]{1,0:T(8,128)S(1)} collective-permute-done((f32[64,832]{1,0:T(8,128)S(1)}, f32[64,832]{1,0:T(8,128)S(1)}, u32[]{:S(2)}, u32[]{:S(2)}) %collective-permute-start.28) | collective-permute-done | bytes 213024 | tf_op jit(solution)/shard_map/ppermute | solution.py:33
  625.4 7.5 %collective-permute-done.29 = f32[64,832]{1,0:T(8,128)S(1)} collective-permute-done((f32[64,832]{1,0:T(8,128)S(1)}, f32[64,832]{1,0:T(8,128)S(1)}, u32[]{:S(2)}, u32[]{:S(2)}) %collective-permute-start.29) | collective-permute-done | bytes 213024 | tf_op jit(solution)/shard_map/ppermute | solution.py:33
  635.3 3.0 collective-permute-done.30
  638.5 3.5 collective-permute-done.31
  642.1 2.8 collective-permute-start.32
  (765 shorter events, 371.5 us)
Async XLA Ops:
  0.6 17.5 %copy-start = (bf16[512,2048]{1,0:T(8,128)(2,1)S(1)}, bf16[512,2048]{1,0:T(8,128)(2,1)}, u32[]{:S(2)}) copy-start(bf16[512,2048]{1,0:T(8,128)(2,1)} %param.15) | copy-start | bytes 6291460
  2.1 3.8 collective-permute-start
  3.3 8.6 %copy-start.47 = (s32[16384]{0:T(1024)}, s32[16384]{0:T(1024)S(1)}, u32[]{:S(2)}) copy-start(s32[16384]{0:T(1024)S(1)} %add_bitcast_fusion.1) | copy-start | bytes 196612
  5.9 6.1 collective-permute-start.1
  7.4 10.7 %copy-start.39 = (f32[512,64]{0,1:T(8,128)S(1)}, f32[512,64]{0,1:T(8,128)}, u32[]{:S(2)}) copy-start(f32[512,64]{0,1:T(8,128)} %param.16) | copy-start | bytes 393220
  11.9 5.3 collective-permute-start.2
  18.7 11.6 %collective-permute-start.3 = (f32[64,2048]{1,0:T(8,128)S(1)}, f32[64,2048]{1,0:T(8,128)S(1)}, u32[]{:S(2)}, u32[]{:S(2)}) collective-permute-start(f32[64,2048]{1,0:T(8,128)S(1)} %fusion.221), channel_id=1, source_target_pairs={{0,1},{1,0},{2,3},{3,2},{4,5},{5,4},{6,7},{7,6},{8,9},{9,8},{10,11... | collective-permute-start | bytes 1572872 | tf_op jit(solution)/shard_map/ppermute | solution.py:33
  29.2 3.6 copy-start.49
  30.4 11.0 %collective-permute-start.4 = (f32[64,2048]{1,0:T(8,128)S(1)}, f32[64,2048]{1,0:T(8,128)S(1)}, u32[]{:S(2)}, u32[]{:S(2)}) collective-permute-start(f32[64,2048]{1,0:T(8,128)S(1)} %add.331), channel_id=1, source_target_pairs={{0,2},{1,3},{2,0},{3,1},{4,6},{5,7},{6,4},{7,5},{8,10},{9,11},{10,... | collective-permute-start | bytes 1572872 | tf_op jit(solution)/shard_map/ppermute | solution.py:33
  41.4 12.6 %collective-permute-start.5 = (f32[64,2048]{1,0:T(8,128)S(1)}, f32[64,2048]{1,0:T(8,128)}, u32[]{:S(2)}, u32[]{:S(2)}) collective-permute-start(f32[64,2048]{1,0:T(8,128)S(1)} %add.332), channel_id=1, source_target_pairs={{0,4},{1,5},{2,6},{3,7},{4,0},{5,1},{6,2},{7,3},{8,12},{9,13},{10,... | collective-permute-start | bytes 1572872 | tf_op jit(solution)/shard_map/ppermute | solution.py:33
  52.3 13.9 %copy-start.44 = (f32[64]{0:T(128)S(1)}, f32[64]{0:T(128)}, u32[]{:S(2)}) copy-start(f32[64]{0:T(128)} %param.20) | copy-start | bytes 772
  52.3 13.9 %copy-start.53 = (f32[64]{0:T(128)S(1)}, f32[64]{0:T(128)}, u32[]{:S(2)}) copy-start(f32[64]{0:T(128)} %param.19) | copy-start | bytes 772
  55.1 19.9 %copy-start.35 = (f32[64,2048]{1,0:T(8,128)}, f32[64,2048]{1,0:T(8,128)S(1)}, u32[]{:S(2)}) copy-start(f32[64,2048]{1,0:T(8,128)S(1)} %add.333) | copy-start | bytes 1572868
  56.5 15.5 %collective-permute-start.6 = (f32[128,1280]{1,0:T(8,128)S(1)}, f32[128,1280]{1,0:T(8,128)S(1)}, u32[]{:S(2)}, u32[]{:S(2)}) collective-permute-start(f32[128,1280]{1,0:T(8,128)S(1)} %get-tuple-element.601), channel_id=1, source_target_pairs={{0,8},{8,16},{16,24},{24,32},{32,40},{40,48},{48,56},{56,64},{64,7... | collective-permute-start | bytes 1966088 | tf_op jit(solution)/shard_map/ppermute | solution.py:19
  58.4 15.3 %collective-permute-start.7 = (f32[128,1280]{1,0:T(8,128)S(1)}, f32[128,1280]{1,0:T(8,128)S(1)}, u32[]{:S(2)}, u32[]{:S(2)}) collective-permute-start(f32[128,1280]{1,0:T(8,128)S(1)} %get-tuple-element.602), channel_id=1, source_target_pairs={{8,0},{16,8},{24,16},{32,24},{40,32},{48,40},{56,48},{64,56},{72,6... | collective-permute-start | bytes 1966088 | tf_op jit(solution)/shard_map/ppermute | solution.py:19
  77.2 2.4 copy-start.6
  92.1 2.4 copy-start.6
  107.0 2.4 copy-start.6
  136.9 2.4 copy-start.6
  153.2 12.4 %collective-permute-start.8 = (f32[64,1280]{1,0:T(8,128)}, f32[64,1280]{1,0:T(8,128)S(1)}, u32[]{:S(2)}, u32[]{:S(2)}) collective-permute-start(f32[64,1280]{1,0:T(8,128)} %get-tuple-element.597), channel_id=1, source_target_pairs={{0,8},{8,16},{16,24},{24,32},{32,40},{40,48},{48,56},{56,64},{64,7... | collective-permute-start | bytes 983048 | tf_op jit(solution)/shard_map/ppermute | solution.py:19
  155.1 12.0 %collective-permute-start.9 = (f32[64,1280]{1,0:T(8,128)S(1)}, f32[64,1280]{1,0:T(8,128)}, u32[]{:S(2)}, u32[]{:S(2)}) collective-permute-start(f32[64,1280]{1,0:T(8,128)S(1)} %get-tuple-element.598), channel_id=1, source_target_pairs={{8,0},{16,8},{24,16},{32,24},{40,32},{48,40},{56,48},{64,56},{72,6... | collective-permute-start | bytes 983048 | tf_op jit(solution)/shard_map/ppermute | solution.py:19
  170.9 2.4 copy-start.7
  185.8 2.4 copy-start.7
  200.8 2.4 copy-start.7
  230.6 2.4 copy-start.7
  246.2 9.1 %collective-permute-start.10 = (bf16[64,256]{1,0:T(8,128)(2,1)S(1)}, bf16[64,256]{1,0:T(8,128)(2,1)S(1)}, u32[]{:S(2)}, u32[]{:S(2)}) collective-permute-start(bf16[64,256]{1,0:T(8,128)(2,1)S(1)} %slice.370), channel_id=1, source_target_pairs={{0,8},{8,16},{16,24},{24,32},{32,40},{40,48},{48,56},{56,64},{64,7... | collective-permute-start | bytes 98312 | tf_op jit(solution)/shard_map/ppermute | solution.py:19
  294.6 26.4 %copy-start.40 = (f32[512,64]{0,1:T(8,128)S(1)}, f32[512,64]{0,1:T(8,128)}, u32[]{:S(2)}) copy-start(f32[512,64]{0,1:T(8,128)} %param.16) | copy-start | bytes 393220
  294.7 1.6 collective-permute-start.11
  296.4 7.7 %collective-permute-start.12 = (f32[64,832]{1,0:T(8,128)S(1)}, f32[64,832]{1,0:T(8,128)S(1)}, u32[]{:S(2)}, u32[]{:S(2)}) collective-permute-start(f32[64,832]{1,0:T(8,128)S(1)} %fusion.272), channel_id=1, source_target_pairs={{0,16},{8,24},{16,0},{24,8},{32,48},{40,56},{48,32},{56,40},{64,80... | collective-permute-start | bytes 638984 | tf_op jit(solution)/shard_map/ppermute | solution.py:33
  304.2 8.4 %collective-permute-start.13 = (f32[64,832]{1,0:T(8,128)S(1)}, f32[64,832]{1,0:T(8,128)S(1)}, u32[]{:S(2)}, u32[]{:S(2)}) collective-permute-start(f32[64,832]{1,0:T(8,128)S(1)} %add.350), channel_id=1, source_target_pairs={{0,32},{8,40},{16,48},{24,56},{32,0},{40,8},{48,16},{56,24},{64,96... | collective-permute-start | bytes 638984 | tf_op jit(solution)/shard_map/ppermute | solution.py:33
  312.6 7.6 %collective-permute-start.14 = (f32[64,832]{1,0:T(8,128)S(1)}, f32[64,832]{1,0:T(8,128)S(1)}, u32[]{:S(2)}, u32[]{:S(2)}) collective-permute-start(f32[64,832]{1,0:T(8,128)S(1)} %add.351), channel_id=1, source_target_pairs={{0,64},{8,72},{16,80},{24,88},{32,96},{40,104},{48,112},{56,120},{... | collective-permute-start | bytes 638984 | tf_op jit(solution)/shard_map/ppermute | solution.py:33
  320.2 14.5 %copy-start.43 = (f32[64,832]{1,0:T(8,128)}, f32[64,832]{1,0:T(8,128)S(1)}, u32[]{:S(2)}) copy-start(f32[64,832]{1,0:T(8,128)S(1)} %add.352) | copy-start | bytes 638980
  321.5 14.7 %copy-start.37 = (f32[512,64]{0,1:T(8,128)}, f32[512,64]{0,1:T(8,128)S(1)}, u32[]{:S(2)}) copy-start(f32[512,64]{0,1:T(8,128)S(1)} %fusion.212) | copy-start | bytes 393220
  321.8 3.8 collective-permute-start.15
  325.6 3.9 collective-permute-start.16
  329.5 5.2 collective-permute-start.17
  334.8 3.1 copy-start.45
  335.7 10.6 %copy-start.50 = (s32[16384]{0:T(1024)S(1)}, s32[16384]{0:T(1024)}, u32[]{:S(2)}) copy-start(s32[16384]{0:T(1024)} %copy-done.49) | copy-start | bytes 196612
  336.2 9.3 %collective-permute-start.18 = (f32[64,2048]{1,0:T(8,128)S(1)}, f32[64,2048]{1,0:T(8,128)S(1)}, u32[]{:S(2)}, u32[]{:S(2)}) collective-permute-start(f32[64,2048]{1,0:T(8,128)S(1)} %fusion.222), channel_id=1, source_target_pairs={{0,1},{1,0},{2,3},{3,2},{4,5},{5,4},{6,7},{7,6},{8,9},{9,8},{10,11... | collective-permute-start | bytes 1572872 | tf_op jit(solution)/shard_map/ppermute | solution.py:33
  345.5 13.0 %collective-permute-start.19 = (f32[64,2048]{1,0:T(8,128)S(1)}, f32[64,2048]{1,0:T(8,128)S(1)}, u32[]{:S(2)}, u32[]{:S(2)}) collective-permute-start(f32[64,2048]{1,0:T(8,128)S(1)} %add.357), channel_id=1, source_target_pairs={{0,2},{1,3},{2,0},{3,1},{4,6},{5,7},{6,4},{7,5},{8,10},{9,11},{10,... | collective-permute-start | bytes 1572872 | tf_op jit(solution)/shard_map/ppermute | solution.py:33
  352.7 8.8 %copy-start.48 = (s32[16384]{0:T(1024)S(1)}, s32[16384]{0:T(1024)}, u32[]{:S(2)}) copy-start(s32[16384]{0:T(1024)} %copy-done.47) | copy-start | bytes 196612
  358.6 10.8 %collective-permute-start.20 = (f32[64,2048]{1,0:T(8,128)S(1)}, f32[64,2048]{1,0:T(8,128)S(1)}, u32[]{:S(2)}, u32[]{:S(2)}) collective-permute-start(f32[64,2048]{1,0:T(8,128)S(1)} %add.358), channel_id=1, source_target_pairs={{0,4},{1,5},{2,6},{3,7},{4,0},{5,1},{6,2},{7,3},{8,12},{9,13},{10,... | collective-permute-start | bytes 1572872 | tf_op jit(solution)/shard_map/ppermute | solution.py:33
  369.4 17.4 %copy-start.33 = (f32[64,2048]{1,0:T(8,128)}, f32[64,2048]{1,0:T(8,128)S(1)}, u32[]{:S(2)}) copy-start(f32[64,2048]{1,0:T(8,128)S(1)} %add.359) | copy-start | bytes 1572868
  369.5 16.0 %collective-permute-start.21 = (f32[128,1280]{1,0:T(8,128)S(1)}, f32[128,1280]{1,0:T(8,128)S(1)}, u32[]{:S(2)}, u32[]{:S(2)}) collective-permute-start(f32[128,1280]{1,0:T(8,128)S(1)} %get-tuple-element.599), channel_id=1, source_target_pairs={{0,8},{8,16},{16,24},{24,32},{32,40},{40,48},{48,56},{56,64},{64,7... | collective-permute-start | bytes 1966088 | tf_op jit(solution)/shard_map/ppermute | solution.py:19
  371.5 15.3 %collective-permute-start.22 = (f32[128,1280]{1,0:T(8,128)S(1)}, f32[128,1280]{1,0:T(8,128)S(1)}, u32[]{:S(2)}, u32[]{:S(2)}) collective-permute-start(f32[128,1280]{1,0:T(8,128)S(1)} %get-tuple-element.600), channel_id=1, source_target_pairs={{8,0},{16,8},{24,16},{32,24},{40,32},{48,40},{56,48},{64,56},{72,6... | collective-permute-start | bytes 1966088 | tf_op jit(solution)/shard_map/ppermute | solution.py:19
  404.0 2.4 copy-start.11
  433.9 2.4 copy-start.11
  465.2 12.4 %collective-permute-start.23 = (f32[64,1280]{1,0:T(8,128)}, f32[64,1280]{1,0:T(8,128)S(1)}, u32[]{:S(2)}, u32[]{:S(2)}) collective-permute-start(f32[64,1280]{1,0:T(8,128)} %get-tuple-element.595), channel_id=1, source_target_pairs={{0,8},{8,16},{16,24},{24,32},{32,40},{40,48},{48,56},{56,64},{64,7... | collective-permute-start | bytes 983048 | tf_op jit(solution)/shard_map/ppermute | solution.py:19
  467.1 12.0 %collective-permute-start.24 = (f32[64,1280]{1,0:T(8,128)S(1)}, f32[64,1280]{1,0:T(8,128)}, u32[]{:S(2)}, u32[]{:S(2)}) collective-permute-start(f32[64,1280]{1,0:T(8,128)S(1)} %get-tuple-element.596), channel_id=1, source_target_pairs={{8,0},{16,8},{24,16},{32,24},{40,32},{48,40},{56,48},{64,56},{72,6... | collective-permute-start | bytes 983048 | tf_op jit(solution)/shard_map/ppermute | solution.py:19
  482.4 78.7 %copy-start.46 = (f32[32,128]{1,0:T(8,128)S(1)}, f32[32,128]{1,0:T(8,128)}, u32[]{:S(2)}) copy-start(f32[32,128]{1,0:T(8,128)} %copy-done.45) | copy-start | bytes 49156
  482.4 78.7 %copy-start.51 = (pred[32,128]{1,0:T(8,128)(4,1)S(1)}, pred[32,128]{1,0:T(8,128)(4,1)}, u32[]{:S(2)}) copy-start(pred[32,128]{1,0:T(8,128)(4,1)} %get-tuple-element.578) | copy-start | bytes 12292
  482.9 2.4 copy-start.12
  497.8 2.4 copy-start.12
  512.7 2.4 copy-start.12
  542.6 2.4 copy-start.12
  559.0 9.1 %collective-permute-start.25 = (bf16[64,256]{1,0:T(8,128)(2,1)S(1)}, bf16[64,256]{1,0:T(8,128)(2,1)S(1)}, u32[]{:S(2)}, u32[]{:S(2)}) collective-permute-start(bf16[64,256]{1,0:T(8,128)(2,1)S(1)} %slice.387), channel_id=1, source_target_pairs={{0,8},{8,16},{16,24},{24,32},{32,40},{40,48},{48,56},{56,64},{64,7... | collective-permute-start | bytes 98312 | tf_op jit(solution)/shard_map/ppermute | solution.py:19
  607.4 26.4 %copy-start.38 = (f32[512,64]{0,1:T(8,128)S(1)}, f32[512,64]{0,1:T(8,128)}, u32[]{:S(2)}) copy-start(f32[512,64]{0,1:T(8,128)} %copy-done.37) | copy-start | bytes 393220
  607.5 1.6 collective-permute-start.26
  609.2 7.7 %collective-permute-start.27 = (f32[64,832]{1,0:T(8,128)S(1)}, f32[64,832]{1,0:T(8,128)S(1)}, u32[]{:S(2)}, u32[]{:S(2)}) collective-permute-start(f32[64,832]{1,0:T(8,128)S(1)} %fusion.271), channel_id=1, source_target_pairs={{0,16},{8,24},{16,0},{24,8},{32,48},{40,56},{48,32},{56,40},{64,80... | collective-permute-start | bytes 638984 | tf_op jit(solution)/shard_map/ppermute | solution.py:33
  616.9 8.4 %collective-permute-start.28 = (f32[64,832]{1,0:T(8,128)S(1)}, f32[64,832]{1,0:T(8,128)S(1)}, u32[]{:S(2)}, u32[]{:S(2)}) collective-permute-start(f32[64,832]{1,0:T(8,128)S(1)} %add.366), channel_id=1, source_target_pairs={{0,32},{8,40},{16,48},{24,56},{32,0},{40,8},{48,16},{56,24},{64,96... | collective-permute-start | bytes 638984 | tf_op jit(solution)/shard_map/ppermute | solution.py:33
  625.4 7.6 %collective-permute-start.29 = (f32[64,832]{1,0:T(8,128)S(1)}, f32[64,832]{1,0:T(8,128)S(1)}, u32[]{:S(2)}, u32[]{:S(2)}) collective-permute-start(f32[64,832]{1,0:T(8,128)S(1)} %add.367), channel_id=1, source_target_pairs={{0,64},{8,72},{16,80},{24,88},{32,96},{40,104},{48,112},{56,120},{... | collective-permute-start | bytes 638984 | tf_op jit(solution)/shard_map/ppermute | solution.py:33
  634.5 3.8 collective-permute-start.30
  638.3 3.7 collective-permute-start.31
  642.1 5.2 collective-permute-start.32
  (135 other events, 212.4 us)
